TPU v7x, 512 devices: a whole 4x8x8 slice. The times are simulated.
512 devices in a mesh: space: 64 (over x, y, core), chan: 8 (over z).
Axes of the slice: x: 4, y: 8, z: 8, core: 2. Of those that a mesh axis runs over, the one named last changes fastest.
Arguments:
- features: bfloat16 [128, 64, 4096], P('space', 'chan'), may hold values from -6 to 6
- conv_weight: bfloat16 [128, 9, 64], P('chan'), may hold values from -0.25 to 0.25
- down_weight: bfloat16 [128, 4, 128], P('chan'), may hold values from -0.25 to 0.25
- cotangent: bfloat16 [128, 128, 1024], P('space', 'chan'), may hold values from -16 to 16
- partner: int32 [128, 4], P('space'), may hold values from 0 to 511, as said below
- orientation: int32 [128, 4], P('space'), may hold values from 0 to 1, as said below
Outputs:
- pooled: bfloat16 [128, 128, 1024], P('space', 'chan')
- features_grad: bfloat16 [128, 64, 4096], P('space', 'chan')
- conv_grad: float32 [128, 9, 64], P('chan')
- down_grad: float32 [128, 4, 128], P('chan')
Inputs may be any that keep to these rules, and one draw needn't show every extreme that they name: Bordering is mutual: the slot at partner[t, e] has partner 4 t + e; no edge borders itself; every slot 0 to 511 appears exactly once. `orientation`: both edges of a bordering pair carry the same value.
All inputs are finite; a program needn't handle non-finite values.
Results may differ from a plain program's by a relative error of at most 0.0049.
Values may be sent and summed in bfloat16 or wider, within the bound.
No kernel may reach another device: no remote copies, remote signals or barrier semaphores. Data moves between devices by JAX's collectives and lax.ppermute only.
A program may use at most 64 MiB of HBM per device.

v0:
```python
import jax
import jax.numpy as jnp
from jax import lax
from jax.sharding import PartitionSpec as P

S = 64
F32 = jnp.float32
BF16 = jnp.bfloat16


def edge_strips(values):
    return jnp.stack(
        [values[..., 0, :], values[..., :, -1], values[..., -1, :], values[..., :, 0]], axis=-3
    )


def rim_strips(padded):
    return jnp.stack(
        [padded[..., 0, 1:-1], padded[..., 1:-1, -1], padded[..., -1, 1:-1], padded[..., 1:-1, 0]],
        axis=-3,
    )


def bordering(strips, partner, orientation):
    flat = strips.reshape((-1,) + strips.shape[2:])
    picked = jnp.take(flat, partner.reshape(-1), axis=0)
    picked = picked.reshape(partner.shape + strips.shape[2:])
    return jnp.where((orientation == 1)[..., None, None], picked[..., ::-1], picked)


def pad_tile(values, halo_strips):
    tile_side = values.shape[-1]
    widths = [(0, 0)] * (values.ndim - 2) + [(1, 1), (1, 1)]
    padded = jnp.pad(values, widths)
    padded = padded.at[..., 0, 1 : tile_side + 1].set(halo_strips[..., 0, :, :])
    padded = padded.at[..., 1 : tile_side + 1, tile_side + 1].set(halo_strips[..., 1, :, :])
    padded = padded.at[..., tile_side + 1, 1 : tile_side + 1].set(halo_strips[..., 2, :, :])
    return padded.at[..., 1 : tile_side + 1, 0].set(halo_strips[..., 3, :, :])


def pad_cat(values, halo):
    zero = jnp.zeros(values.shape[:2] + (1, 1), values.dtype)
    top = jnp.concatenate([zero, halo[:, 0, :, None, :], zero], axis=3)
    bottom = jnp.concatenate([zero, halo[:, 2, :, None, :], zero], axis=3)
    middle = jnp.concatenate([halo[:, 3, :, :, None], values, halo[:, 1, :, :, None]], axis=3)
    return jnp.concatenate([top, middle, bottom], axis=2)


def add_edges(interior, returned):
    n = interior.shape[-1]
    none = ((0, 0), (0, 0))
    rows = jnp.pad(returned[:, 0, :, None, :], none + ((0, n - 1), (0, 0))) + jnp.pad(
        returned[:, 2, :, None, :], none + ((n - 1, 0), (0, 0))
    )
    cols = jnp.pad(returned[:, 3, :, :, None], none + ((0, 0), (0, n - 1))) + jnp.pad(
        returned[:, 1, :, :, None], none + ((0, 0), (n - 1, 0))
    )
    return interior + (rows + cols)


def unfold(padded, height, width):
    taps = [
        padded[..., row_shift : row_shift + height, col_shift : col_shift + width]
        for row_shift in range(3)
        for col_shift in range(3)
    ]
    return jnp.stack(taps, axis=-4)


def fold_taps(taps):
    total = None
    for row_shift in range(3):
        for col_shift in range(3):
            piece = taps[..., 3 * row_shift + col_shift, :, :, :]
            widths = [(0, 0)] * (piece.ndim - 2) + [
                (row_shift, 2 - row_shift),
                (col_shift, 2 - col_shift),
            ]
            placed = jnp.pad(piece, widths)
            total = placed if total is None else total + placed
    return total


def silu_grad(values):
    gate = jax.nn.sigmoid(values)
    return gate * (1.0 + values * (1.0 - gate))


def exchange(parts, axis):
    count = parts[0].shape[0]
    flat = [p.reshape(count, -1) for p in parts]
    sizes = [f.shape[1] for f in flat]
    total = sum(sizes)
    lanes = -(-total // 128) * 128
    buf = jnp.concatenate(flat + [jnp.zeros((count, lanes - total), flat[0].dtype)], axis=1)
    got = lax.all_to_all(buf.reshape(count, lanes // 128, 128), axis, 0, 0, tiled=True)
    got = got.reshape(count, lanes)
    out, start = [], 0
    for p, size in zip(parts, sizes):
        out.append(got[:, start : start + size].reshape(p.shape))
        start += size
    return out


def to_all(value, count):
    return jnp.broadcast_to(value[None], (count,) + value.shape)


def split_wide(value):
    high = lax.reduce_precision(value, exponent_bits=8, mantissa_bits=7)
    return jnp.stack([high, value - high], axis=1).astype(BF16)


def shards(features, conv_weight, down_weight, cotangent, partner, orientation):
    tiles, share, _ = features.shape
    n_chan = lax.axis_size("chan")
    n_space = lax.axis_size("space")
    in_channels = share * n_chan
    out_share = conv_weight.shape[0]
    out_channels = out_share * n_chan
    rows = S // n_chan
    half = S // 2
    conv_cols = conv_weight.shape[1] * conv_weight.shape[2]
    down_cols = down_weight.shape[1] * down_weight.shape[2]

    images = features.reshape(tiles, share, S, S)
    strips = edge_strips(images)
    (strips_all,) = exchange([to_all(strips, n_space)], "space")
    halo = bordering(strips_all.reshape((n_space * tiles,) + strips.shape[1:]), partner, orientation)
    padded = pad_cat(images, halo)

    bands = jnp.stack([padded[:, :, rows * b : rows * b + rows + 2, :] for b in range(n_chan)])
    cot_bands = jnp.moveaxis(cotangent.reshape(tiles, out_share, n_chan, rows // 2 * half), 2, 0)
    weights = jnp.concatenate(
        [conv_weight.reshape(out_share, conv_cols), down_weight.reshape(out_share, down_cols)], axis=1
    )
    band_in, cot_in, w_in = exchange([bands, cot_bands, to_all(weights, n_chan)], "chan")
    block = jnp.moveaxis(band_in, 0, 1).reshape(tiles, in_channels, rows + 2, S + 2)
    grad_band = jnp.moveaxis(cot_in, 0, 1).reshape(tiles, out_channels, rows // 2, half)
    w_full = w_in.reshape(out_channels, conv_cols + down_cols)
    conv_full = w_full[:, :conv_cols].reshape(out_channels, 9, in_channels)
    down_full = w_full[:, conv_cols:].reshape(out_channels, 4, out_channels)

    plain = ("NCHW", "OIHW", "NCHW")
    swapped = ("CNHW", "IOHW", "NCHW")
    w_conv = conv_full.reshape(out_channels, 3, 3, in_channels).transpose(0, 3, 1, 2)
    w_down = down_full.reshape(out_channels, 2, 2, out_channels).transpose(0, 3, 1, 2)
    pre_act = lax.conv_general_dilated(
        block, w_conv, (1, 1), "VALID", dimension_numbers=plain, preferred_element_type=F32
    )
    activated = jax.nn.silu(pre_act).astype(BF16)
    pooled_rows = lax.conv_general_dilated(
        activated, w_down, (2, 2), "VALID", dimension_numbers=plain, preferred_element_type=F32
    ).astype(BF16)
    down_part = lax.conv_general_dilated(
        activated, grad_band, (1, 1), "VALID", rhs_dilation=(2, 2),
        dimension_numbers=swapped, preferred_element_type=F32,
    )
    down_part = down_part.transpose(1, 2, 3, 0).reshape(out_channels, down_cols)
    w_up = jnp.flip(w_down, (2, 3)).transpose(1, 0, 2, 3)
    grad_act = lax.conv_general_dilated(
        grad_band, w_up, (1, 1), ((1, 1), (1, 1)), lhs_dilation=(2, 2),
        dimension_numbers=plain, preferred_element_type=F32,
    )
    grad_pre = (grad_act * silu_grad(pre_act)).astype(BF16)
    conv_part = lax.conv_general_dilated(
        block, grad_pre, (1, 1), "VALID", dimension_numbers=swapped, preferred_element_type=F32
    )
    conv_part = conv_part.transpose(1, 2, 3, 0).reshape(out_channels, conv_cols)
    w_back_conv = jnp.flip(w_conv, (2, 3)).transpose(1, 0, 2, 3)
    grad_block = lax.conv_general_dilated(
        grad_pre, w_back_conv, (1, 1), ((2, 2), (2, 2)), dimension_numbers=plain,
        preferred_element_type=F32,
    )

    pooled_out = jnp.moveaxis(pooled_rows.reshape(tiles, n_chan, out_share, rows // 2 * half), 1, 0)
    grad_out = jnp.moveaxis(
        grad_block.astype(BF16).reshape(tiles, n_chan, share, rows + 2, S + 2), 1, 0
    )
    w_part = jnp.concatenate([conv_part, down_part], axis=1)
    w_part = split_wide(w_part.reshape(n_chan, out_share * (conv_cols + down_cols)))
    pooled_in, grad_in, w_back = exchange([pooled_out, grad_out, w_part], "chan")
    pooled = jnp.moveaxis(pooled_in, 0, 2).reshape(tiles, out_share, half * half)
    w_sum = jnp.sum(w_back.astype(F32), axis=(0, 1))

    g = grad_in.astype(F32)
    main = jnp.moveaxis(g[:, :, :, :rows, :], 0, 2).reshape(tiles, share, S, S + 2)
    extra = jnp.pad(g[:, :, :, rows:, :], ((0, 0), (0, 0), (0, 0), (0, rows - 2), (0, 0)))
    extra = jnp.moveaxis(extra, 0, 2).reshape(tiles, share, S, S + 2)
    grad_padded = jnp.pad(main, ((0, 0), (0, 0), (0, 2), (0, 0))) + jnp.pad(
        extra, ((0, 0), (0, 0), (rows, 0), (0, 0))
    )[:, :, : S + 2, :]

    rims = rim_strips(grad_padded)
    w_len = w_sum.shape[0]
    piece = -(-w_len // n_space)
    w_pieces = jnp.pad(w_sum, (0, piece * n_space - w_len)).reshape(n_space, piece)
    rims_all, w_got = exchange([to_all(rims, n_space), w_pieces], "space")
    w_mine = jnp.sum(w_got, axis=0)
    (w_all,) = exchange([to_all(w_mine, n_space)], "space")
    w_total = w_all.reshape(-1)[:w_len].reshape(out_share, conv_cols + down_cols)

    returned = bordering(rims_all.reshape((n_space * tiles,) + rims.shape[1:]), partner, orientation)
    features_grad = add_edges(grad_padded[:, :, 1:-1, 1:-1], returned).astype(BF16)
    features_grad = features_grad.reshape(tiles, share, S * S)
    grad_scale = float(n_space * tiles * S * S) ** (-0.5)
    conv_grad = w_total[:, :conv_cols].reshape(conv_weight.shape) * grad_scale
    down_grad = w_total[:, conv_cols:].reshape(down_weight.shape) * grad_scale
    return (pooled, features_grad, conv_grad, down_grad)


def solution(mesh):
    placed = (
        P("space", "chan", None),
        P("chan", None, None),
        P("chan", None, None),
        P("space", "chan", None),
        P("space", None),
        P("space", None),
    )
    return jax.shard_map(
        shards,
        mesh=mesh,
        in_specs=placed,
        out_specs=(
            P("space", "chan", None),
            P("space", "chan", None),
            P("chan", None, None),
            P("chan", None, None),
        ),
        check_vma=False,
    )
```

profile of v0, /device:TPU:1, one launch (start us, length us, event | category | flops | bytes accessed | tf_op | source)
XLA Modules:
  0.0 177.8 jit_solution(18265065555759953131)
XLA Ops:
  0.7 1.2 reshape.211
  1.9 0.5 slice_reduce_fusion.1
  2.5 0.9 broadcast_in_dim.65
  3.4 11.6 %all-to-all-start = ((bf16[64,32,128]{2,1,0:T(8,128)(2,1)}), bf16[64,32,128]{2,1,0:T(8,128)(2,1)S(1)}, u32[]{:S(2)}, u32[]{:S(2)}) async-start(bf16[64,32,128]{2,1,0:T(8,128)(2,1)} %broadcast_in_dim.65), calls=%async_computation | async-start | bytes 1048576 | tf_op jit(solution)/shard_map/all_to_all | solution.py:96
  15.5 16.8 %all-to-all-done = bf16[64,32,128]{2,1,0:T(8,128)(2,1)S(1)} async-done(((bf16[64,32,128]{2,1,0:T(8,128)(2,1)}), bf16[64,32,128]{2,1,0:T(8,128)(2,1)S(1)}, u32[]{:S(2)}, u32[]{:S(2)}) %all-to-all-start) | async-done | bytes 524320 | tf_op jit(solution)/shard_map/all_to_all | solution.py:96
  32.3 0.4 reshape_reshape_reshape_reshape.3
  32.7 0.6 gather_fusion
  33.6 0.2 copy.418
  33.8 0.2 copy.417
  34.0 0.3 pad_maximum_fusion.2
  34.3 0.3 fusion.24
  36.1 1.6 stack.48
  37.8 0.4 concatenate.45
  38.2 27.6 %all_to_all.25 = bf16[8,251,128]{2,1,0:T(8,128)(2,1)S(1)} all-to-all(bf16[8,251,128]{2,1,0:T(8,128)(2,1)S(1)} %copy.421), channel_id=1, replica_groups=mesh['space'=64,'chan'=8] {'chan'}, dimensions={0} | all-to-all | bytes 1028096 | tf_op jit(solution)/shard_map/all_to_all | solution.py:96
  65.9 0.3 copy.507
  66.5 0.3 reshape_reshape.13
  67.7 0.6 reshape.219
  68.4 0.4 copy.443
  68.8 0.4 copy.465
  69.2 0.4 pad.36.clone
  69.6 0.5 fusion.7
  70.2 0.3 convolution_select_fusion.1
  70.4 0.4 copy.436
  70.8 0.7 broadcast_select_fusion
  71.8 0.2 convolution_convert_fusion
  72.6 0.6 fusion.18
  73.8 1.8 %fusion.20 = f32[128,3,3,64]{0,3,2,1:T(8,128)S(1)} fusion(bf16[2,64,10,66]{1,0,3,2:T(2,128)(2,1)S(1)} %copy.443, bf16[8,2,64,128]{3,0,2,1:T(8,128)(2,1)S(1)} %fusion.6), kind=kOutput, calls=%fused_computation.52 | convolution fusion | flops 150994944 | bytes 726016 | tf_op jit(solution)/shard_map/transpose | solution.py:169
  76.1 0.2 reshape.229
  76.4 0.3 copy-done.6
  76.7 1.0 fusion
  77.9 0.2 reshape.266
  78.2 0.3 copy.441
  78.4 0.2 copy.442
  78.7 0.4 reshape.226
  79.2 1.3 dynamic-update-slice.1
  80.6 3.9 %dynamic-update-slice.2 = bf16[8,49536]{1,0:T(8,128)(2,1)S(1)} dynamic-update-slice(bf16[8,49536]{1,0:T(8,128)(2,1)S(1)} %dynamic-update-slice.1, bf16[8,34816]{1,0:T(8,128)(2,1)S(1)} %bitcast.159, s32[]{} %constant.88, s32[]{} %constant.90) | dynamic-update-slice | bytes 1114116
  84.5 0.2 dynamic-update-slice.3
  84.9 25.7 %all_to_all.26 = bf16[8,387,128]{2,1,0:T(8,128)(2,1)S(1)} all-to-all(bf16[8,387,128]{2,1,0:T(8,128)(2,1)S(1)} %copy.450), channel_id=1, replica_groups=mesh['space'=64,'chan'=8] {'chan'}, dimensions={0} | all-to-all | bytes 1585152 | tf_op jit(solution)/shard_map/all_to_all | solution.py:96
  110.7 0.4 convert_reduce_fusion
  111.1 0.5 reshape.273
  111.7 0.3 copy.452
  112.1 0.3 copy.454
  112.4 0.2 slice_add_fusion
  113.2 0.7 reshape.236
  114.0 0.3 copy.464
  114.2 0.3 copy.456
  114.7 0.6 broadcast.95
  115.3 1.0 concatenate.48
  116.3 1.3 reshape.237
  117.5 7.0 %all-to-all-start.3 = ((f32[64,35,128]{2,1,0:T(8,128)}), f32[64,35,128]{2,1,0:T(8,128)S(1)}, u32[]{:S(2)}, u32[]{:S(2)}) async-start(f32[64,35,128]{2,1,0:T(8,128)} %reshape.237), calls=%async_computation.3 | async-start | bytes 2621440 | tf_op jit(solution)/shard_map/all_to_all | solution.py:96
  124.6 0.7 reshape.233
  125.2 33.5 %all-to-all-done.3 = f32[64,35,128]{2,1,0:T(8,128)S(1)} async-done(((f32[64,35,128]{2,1,0:T(8,128)}), f32[64,35,128]{2,1,0:T(8,128)S(1)}, u32[]{:S(2)}, u32[]{:S(2)}) %all-to-all-start.3) | async-done | bytes 1146912 | tf_op jit(solution)/shard_map/all_to_all | solution.py:96
  159.0 0.7 concatenate.51
  159.7 6.2 %all-to-all-start.4 = ((f32[64,3,128]{2,1,0:T(4,128)}), f32[64,3,128]{2,1,0:T(4,128)S(1)}, u32[]{:S(2)}, u32[]{:S(2)}) async-start(f32[64,3,128]{2,1,0:T(4,128)} %concatenate.51), calls=%async_computation.4 | async-start | bytes 262144 | tf_op jit(solution)/shard_map/all_to_all | solution.py:96
  165.9 2.2 %reshape_reshape_reshape.3 = f32[512,8,64]{2,1,0:T(8,128)} reshape(f32[64,4096]{1,0:T(8,128)S(1)} %slice.215) | data formatting | bytes 2097152 | tf_op jit(solution)/shard_map/reshape;reshape;reshape | solution.py:25
  168.0 2.1 %gather_fusion.1 = f32[8,8,64]{2,1,0:T(8,128)S(1)} fusion(f32[512,8,64]{2,1,0:T(8,128)} %reshape_reshape_reshape.3, s32[1024]{0:T(1024)S(1)} %pad_clamp_fusion), kind=kCustom, calls=%fused_computation.1 | custom fusion | bytes 32800 | tf_op jit(solution)/shard_map/jit(_take)/gather | solution.py:26
  170.4 0.3 copy.458
  170.8 0.3 copy.459
  171.1 0.3 fusion.5
  171.4 0.3 copy.460
  171.7 0.9 reshape.239
  172.7 3.5 %all-to-all-done.4 = f32[64,3,128]{2,1,0:T(4,128)S(1)} async-done(((f32[64,3,128]{2,1,0:T(4,128)}), f32[64,3,128]{2,1,0:T(4,128)S(1)}, u32[]{:S(2)}, u32[]{:S(2)}) %all-to-all-start.4) | async-done | bytes 98336 | tf_op jit(solution)/shard_map/all_to_all | solution.py:96
  176.4 0.6 mul.40
  177.1 0.7 copy.461
  (116 shorter events, 7.8 us)
Async XLA Ops:
  0.6 14.4 %copy-start.4 = (s32[2,4]{1,0:T(2,128)S(1)}, s32[2,4]{1,0:T(2,128)}, u32[]{:S(2)}) copy-start(s32[2,4]{1,0:T(2,128)} %param.10) | copy-start | bytes 100
  0.6 14.5 %copy-start.2 = (bf16[16,4,128]{2,1,0:T(4,128)(2,1)S(1)}, bf16[16,4,128]{2,1,0:T(4,128)(2,1)}, u32[]{:S(2)}) copy-start(bf16[16,4,128]{2,1,0:T(4,128)(2,1)} %param.8) | copy-start | bytes 49156
  0.7 14.5 %copy-start.1 = (bf16[16,9,64]{2,0,1:T(8,128)(2,1)S(1)}, bf16[16,9,64]{2,0,1:T(8,128)(2,1)}, u32[]{:S(2)}) copy-start(bf16[16,9,64]{2,0,1:T(8,128)(2,1)} %param.7) | copy-start | bytes 55300
  1.9 13.6 %copy-start = (bf16[2,16,1024]{2,1,0:T(8,128)(2,1)S(1)}, bf16[2,16,1024]{2,1,0:T(8,128)(2,1)}, u32[]{:S(2)}) copy-start(bf16[2,16,1024]{2,1,0:T(8,128)(2,1)} %param.9) | copy-start | bytes 196612
  1.9 13.6 %copy-start.5 = (s32[2,4]{1,0:T(2,128)S(1)}, s32[2,4]{1,0:T(2,128)}, u32[]{:S(2)}) copy-start(s32[2,4]{1,0:T(2,128)} %param.11) | copy-start | bytes 100
  3.4 28.9 %all-to-all-start = ((bf16[64,32,128]{2,1,0:T(8,128)(2,1)}), bf16[64,32,128]{2,1,0:T(8,128)(2,1)S(1)}, u32[]{:S(2)}, u32[]{:S(2)}) async-start(bf16[64,32,128]{2,1,0:T(8,128)(2,1)} %broadcast_in_dim.65), calls=%async_computation | async-start | bytes 1048576 | tf_op jit(solution)/shard_map/all_to_all | solution.py:96
  68.8 1.3 copy-start.3
  70.1 0.7 copy-start.7
  76.0 0.7 copy-start.6
  117.5 41.2 %all-to-all-start.3 = ((f32[64,35,128]{2,1,0:T(8,128)}), f32[64,35,128]{2,1,0:T(8,128)S(1)}, u32[]{:S(2)}, u32[]{:S(2)}) async-start(f32[64,35,128]{2,1,0:T(8,128)} %reshape.237), calls=%async_computation.3 | async-start | bytes 2621440 | tf_op jit(solution)/shard_map/all_to_all | solution.py:96
  159.7 16.5 %all-to-all-start.4 = ((f32[64,3,128]{2,1,0:T(4,128)}), f32[64,3,128]{2,1,0:T(4,128)S(1)}, u32[]{:S(2)}, u32[]{:S(2)}) async-start(f32[64,3,128]{2,1,0:T(4,128)} %concatenate.51), calls=%async_computation.4 | async-start | bytes 262144 | tf_op jit(solution)/shard_map/all_to_all | solution.py:96
where the time goes:
time: 178 us
  waiting for transfers between devices  53.8 us (30%)
  blocking collectives  53.3 us (30%)
  local copies, waits for them, and re-layouts  36.3 us (20%)
  starting transfers between devices  24.8 us (14%)
  matrix products  4.61 us (3%)
  other arithmetic  3.35 us (2%)
    all_to_all x3, waiting for transfers between devices, exchange(): lax.all_to_all(buf.reshape(count, lanes // 128, 128), axis, 0, 0, tiled=T...  53.8 us
    all_to_all x2, blocking collectives, exchange(): lax.all_to_all(buf.reshape(count, lanes // 128, 128), axis, 0, 0, tiled=T...  53.3 us
    all_to_all x3, starting transfers between devices, exchange(): lax.all_to_all(buf.reshape(count, lanes // 128, 128), axis, 0, 0, tiled=T...  24.8 us
    unnamed x32, local copies, waits for them, and re-layouts  7.92 us
  transfers between devices with their start and end apart: 3, of which 3 were waited for; matrix products, arithmetic and copies ran while one was open for 4% of the time, Pallas kernels for 0%

commit v1 on v0

--- a/solution.py
+++ b/solution.py
@@ -123,6 +123,10 @@
     conv_cols = conv_weight.shape[1] * conv_weight.shape[2]
     down_cols = down_weight.shape[1] * down_weight.shape[2]
 
+    weights = jnp.concatenate(
+        [conv_weight.reshape(out_share, conv_cols), down_weight.reshape(out_share, down_cols)], axis=1
+    )
+
     images = features.reshape(tiles, share, S, S)
     strips = edge_strips(images)
     (strips_all,) = exchange([to_all(strips, n_space)], "space")
@@ -131,9 +135,6 @@
 
     bands = jnp.stack([padded[:, :, rows * b : rows * b + rows + 2, :] for b in range(n_chan)])
     cot_bands = jnp.moveaxis(cotangent.reshape(tiles, out_share, n_chan, rows // 2 * half), 2, 0)
-    weights = jnp.concatenate(
-        [conv_weight.reshape(out_share, conv_cols), down_weight.reshape(out_share, down_cols)], axis=1
-    )
     band_in, cot_in, w_in = exchange([bands, cot_bands, to_all(weights, n_chan)], "chan")
     block = jnp.moveaxis(band_in, 0, 1).reshape(tiles, in_channels, rows + 2, S + 2)
     grad_band = jnp.moveaxis(cot_in, 0, 1).reshape(tiles, out_channels, rows // 2, half)
@@ -195,12 +196,13 @@
     w_len = w_sum.shape[0]
     piece = -(-w_len // n_space)
     w_pieces = jnp.pad(w_sum, (0, piece * n_space - w_len)).reshape(n_space, piece)
-    rims_all, w_got = exchange([to_all(rims, n_space), w_pieces], "space")
-    w_mine = jnp.sum(w_got, axis=0)
+    rims_all, w_got = exchange([to_all(rims.astype(BF16), n_space), split_wide(w_pieces)], "space")
+    w_mine = jnp.sum(w_got.astype(F32), axis=(0, 1))
     (w_all,) = exchange([to_all(w_mine, n_space)], "space")
     w_total = w_all.reshape(-1)[:w_len].reshape(out_share, conv_cols + down_cols)
 
     returned = bordering(rims_all.reshape((n_space * tiles,) + rims.shape[1:]), partner, orientation)
+    returned = returned.astype(F32)
     features_grad = add_edges(grad_padded[:, :, 1:-1, 1:-1], returned).astype(BF16)
     features_grad = features_grad.reshape(tiles, share, S * S)
     grad_scale = float(n_space * tiles * S * S) ** (-0.5)

time: 178 us -> 162 us (0.910)
  waiting for transfers between devices: 53.8 us -> 42.3 us
  local copies, waits for them, and re-layouts: 36.3 us -> 31.7 us
    all_to_all x3, waiting for transfers between devices: 53.8 us -> 42.3 us  [exchange(): lax.all_to_all(buf.reshape(count, lanes // 128, 128), axis, 0, 0, tiled=T...]
  transfers between devices with their start and end apart: 3 -> 3, of which waited for: 3 -> 3; matrix products, arithmetic and copies ran while one was open for 4% -> 3% of each run, Pallas kernels for 0% -> 0%
where the time goes in v1:
time: 162 us
  blocking collectives  53.3 us (33%)
  waiting for transfers between devices  42.3 us (26%)
  local copies, waits for them, and re-layouts  31.7 us (20%)
  starting transfers between devices  24.9 us (15%)
  matrix products  4.61 us (3%)
  other arithmetic  3.42 us (2%)
  between operations  1.62 us (1%)
    all_to_all x2, blocking collectives, exchange(): lax.all_to_all(buf.reshape(count, lanes // 128, 128), axis, 0, 0, tiled=T...  53.3 us
    all_to_all x3, waiting for transfers between devices, exchange(): lax.all_to_all(buf.reshape(count, lanes // 128, 128), axis, 0, 0, tiled=T...  42.3 us
    all_to_all x3, starting transfers between devices, exchange(): lax.all_to_all(buf.reshape(count, lanes // 128, 128), axis, 0, 0, tiled=T...  24.9 us
    unnamed x32, local copies, waits for them, and re-layouts  7.83 us
  transfers between devices with their start and end apart: 3, of which 3 were waited for; matrix products, arithmetic and copies ran while one was open for 3% of the time, Pallas kernels for 0%

profile of v1, /device:TPU:1, one launch (start us, length us, event | category | flops | bytes accessed | tf_op | source)
XLA Modules:
  0.0 161.9 jit_solution(10815456974806512069)
XLA Ops:
  0.6 1.2 reshape.240
  1.8 0.5 slice_reduce_fusion.1
  2.5 0.9 broadcast_in_dim.54
  3.4 11.6 %all-to-all-start = ((bf16[64,32,128]{2,1,0:T(8,128)(2,1)}), bf16[64,32,128]{2,1,0:T(8,128)(2,1)S(1)}, u32[]{:S(2)}, u32[]{:S(2)}) async-start(bf16[64,32,128]{2,1,0:T(8,128)(2,1)} %broadcast_in_dim.54), calls=%async_computation | async-start | bytes 1048576 | tf_op jit(solution)/shard_map/all_to_all | solution.py:96
  15.5 16.8 %all-to-all-done = bf16[64,32,128]{2,1,0:T(8,128)(2,1)S(1)} async-done(((bf16[64,32,128]{2,1,0:T(8,128)(2,1)}), bf16[64,32,128]{2,1,0:T(8,128)(2,1)S(1)}, u32[]{:S(2)}, u32[]{:S(2)}) %all-to-all-start) | async-done | bytes 524320 | tf_op jit(solution)/shard_map/all_to_all | solution.py:96
  32.3 0.4 reshape_reshape_reshape_reshape.3
  32.7 0.6 gather_fusion
  33.5 0.2 copy.516
  33.8 0.2 copy.515
  34.0 0.3 pad_maximum_fusion.2
  34.3 0.3 fusion.25
  36.1 1.6 stack.62
  37.7 0.4 concatenate.49
  38.2 27.6 %all_to_all.25 = bf16[8,251,128]{2,1,0:T(8,128)(2,1)S(1)} all-to-all(bf16[8,251,128]{2,1,0:T(8,128)(2,1)S(1)} %copy.519), channel_id=1, replica_groups=mesh['space'=64,'chan'=8] {'chan'}, dimensions={0} | all-to-all | bytes 1028096 | tf_op jit(solution)/shard_map/all_to_all | solution.py:96
  65.8 0.3 copy.606
  66.4 0.3 reshape_reshape.13
  67.6 0.6 reshape.249
  68.3 0.4 copy.541
  68.8 0.4 copy.564
  69.2 0.4 pad.36.clone
  69.6 0.5 fusion.7
  70.1 0.3 convolution_select_fusion.1
  70.4 0.4 copy.534
  70.8 0.7 broadcast_select_fusion
  71.8 0.3 convolution_convert_fusion
  72.1 0.2 copy.529
  72.6 0.6 fusion.18
  73.3 0.2 add_multiply_fusion
  73.8 1.8 %fusion.20 = f32[128,3,3,64]{0,3,2,1:T(8,128)S(1)} fusion(bf16[2,64,10,66]{1,0,3,2:T(2,128)(2,1)S(1)} %copy.541, bf16[8,2,64,128]{3,0,2,1:T(8,128)(2,1)S(1)} %fusion.6), kind=kOutput, calls=%fused_computation.52 | convolution fusion | flops 150994944 | bytes 726016 | tf_op jit(solution)/shard_map/transpose | solution.py:170
  76.0 0.2 reshape.259
  76.4 0.3 copy-done.6
  76.7 1.0 fusion
  77.9 0.2 reshape.297
  78.1 0.2 copy.539
  78.4 0.2 copy.540
  78.6 0.4 reshape.256
  79.2 1.3 dynamic-update-slice.1
  80.5 3.9 %dynamic-update-slice.2 = bf16[8,49536]{1,0:T(8,128)(2,1)S(1)} dynamic-update-slice(bf16[8,49536]{1,0:T(8,128)(2,1)S(1)} %dynamic-update-slice.1, bf16[8,34816]{1,0:T(8,128)(2,1)S(1)} %bitcast.157, s32[]{} %constant.71, s32[]{} %constant.73) | dynamic-update-slice | bytes 1114116
  84.4 0.2 dynamic-update-slice.3
  84.8 25.7 %all_to_all.26 = bf16[8,387,128]{2,1,0:T(8,128)(2,1)S(1)} all-to-all(bf16[8,387,128]{2,1,0:T(8,128)(2,1)S(1)} %copy.548), channel_id=1, replica_groups=mesh['space'=64,'chan'=8] {'chan'}, dimensions={0} | all-to-all | bytes 1585152 | tf_op jit(solution)/shard_map/all_to_all | solution.py:96
  110.6 0.4 convert_reduce_fusion
  111.0 0.5 reshape.304
  111.7 0.3 copy.550
  112.1 0.3 copy.552
  112.4 0.2 fusion.30
  113.5 0.3 copy.563
  113.8 0.3 copy.554
  114.2 0.2 concatenate.52
  114.5 1.2 reshape.267
  115.7 7.0 %all-to-all-start.3 = ((bf16[64,37,128]{2,1,0:T(8,128)(2,1)}), bf16[64,37,128]{2,1,0:T(8,128)(2,1)S(1)}, u32[]{:S(2)}, u32[]{:S(2)}) async-start(bf16[64,37,128]{2,1,0:T(8,128)(2,1)} %reshape.267), calls=%async_computation.3 | async-start | bytes 1310720 | tf_op jit(solution)/shard_map/all_to_all | solution.py:96
  122.7 0.7 reshape.263
  123.3 19.4 %all-to-all-done.3 = bf16[64,37,128]{2,1,0:T(8,128)(2,1)S(1)} async-done(((bf16[64,37,128]{2,1,0:T(8,128)(2,1)}), bf16[64,37,128]{2,1,0:T(8,128)(2,1)S(1)}, u32[]{:S(2)}, u32[]{:S(2)}) %all-to-all-start.3) | async-done | bytes 606240 | tf_op jit(solution)/shard_map/all_to_all | solution.py:96
  143.0 0.7 concatenate.55
  143.7 6.3 %all-to-all-start.4 = ((f32[64,3,128]{2,1,0:T(4,128)}), f32[64,3,128]{2,1,0:T(4,128)S(1)}, u32[]{:S(2)}, u32[]{:S(2)}) async-start(f32[64,3,128]{2,1,0:T(4,128)} %concatenate.55), calls=%async_computation.4 | async-start | bytes 262144 | tf_op jit(solution)/shard_map/all_to_all | solution.py:96
  150.0 1.1 reshape_reshape_reshape.3
  151.1 0.6 gather_fusion.1
  151.9 0.3 copy.557
  152.3 0.3 copy.558
  152.6 0.4 fusion.5
  152.9 0.3 copy.559
  153.2 0.9 reshape.270
  154.2 6.1 %all-to-all-done.4 = f32[64,3,128]{2,1,0:T(4,128)S(1)} async-done(((f32[64,3,128]{2,1,0:T(4,128)}), f32[64,3,128]{2,1,0:T(4,128)S(1)}, u32[]{:S(2)}, u32[]{:S(2)}) %all-to-all-start.4) | async-done | bytes 98336 | tf_op jit(solution)/shard_map/all_to_all | solution.py:96
  160.5 0.6 mul.40
  161.2 0.7 copy.560
  (122 shorter events, 7.6 us)
Async XLA Ops:
  1.8 13.2 %copy-start.4 = (s32[2,4]{1,0:T(2,128)S(1)}, s32[2,4]{1,0:T(2,128)}, u32[]{:S(2)}) copy-start(s32[2,4]{1,0:T(2,128)} %param.12) | copy-start | bytes 100
  1.8 13.2 %copy-start.2 = (bf16[16,4,128]{2,1,0:T(4,128)(2,1)S(1)}, bf16[16,4,128]{2,1,0:T(4,128)(2,1)}, u32[]{:S(2)}) copy-start(bf16[16,4,128]{2,1,0:T(4,128)(2,1)} %param.10) | copy-start | bytes 49156
  1.8 13.2 %copy-start.1 = (bf16[16,9,64]{2,0,1:T(8,128)(2,1)S(1)}, bf16[16,9,64]{2,0,1:T(8,128)(2,1)}, u32[]{:S(2)}) copy-start(bf16[16,9,64]{2,0,1:T(8,128)(2,1)} %param.9) | copy-start | bytes 55300
  2.4 13.1 %copy-start = (bf16[2,16,1024]{2,1,0:T(8,128)(2,1)S(1)}, bf16[2,16,1024]{2,1,0:T(8,128)(2,1)}, u32[]{:S(2)}) copy-start(bf16[2,16,1024]{2,1,0:T(8,128)(2,1)} %param.11) | copy-start | bytes 196612
  2.5 13.0 %copy-start.5 = (s32[2,4]{1,0:T(2,128)S(1)}, s32[2,4]{1,0:T(2,128)}, u32[]{:S(2)}) copy-start(s32[2,4]{1,0:T(2,128)} %param.13) | copy-start | bytes 100
  3.4 28.9 %all-to-all-start = ((bf16[64,32,128]{2,1,0:T(8,128)(2,1)}), bf16[64,32,128]{2,1,0:T(8,128)(2,1)S(1)}, u32[]{:S(2)}, u32[]{:S(2)}) async-start(bf16[64,32,128]{2,1,0:T(8,128)(2,1)} %broadcast_in_dim.54), calls=%async_computation | async-start | bytes 1048576 | tf_op jit(solution)/shard_map/all_to_all | solution.py:96
  68.7 1.3 copy-start.3
  70.1 0.7 copy-start.7
  76.0 0.7 copy-start.6
  115.7 27.1 %all-to-all-start.3 = ((bf16[64,37,128]{2,1,0:T(8,128)(2,1)}), bf16[64,37,128]{2,1,0:T(8,128)(2,1)S(1)}, u32[]{:S(2)}, u32[]{:S(2)}) async-start(bf16[64,37,128]{2,1,0:T(8,128)(2,1)} %reshape.267), calls=%async_computation.3 | async-start | bytes 1310720 | tf_op jit(solution)/shard_map/all_to_all | solution.py:96
  143.7 16.6 %all-to-all-start.4 = ((f32[64,3,128]{2,1,0:T(4,128)}), f32[64,3,128]{2,1,0:T(4,128)S(1)}, u32[]{:S(2)}, u32[]{:S(2)}) async-start(f32[64,3,128]{2,1,0:T(4,128)} %concatenate.55), calls=%async_computation.4 | async-start | bytes 262144 | tf_op jit(solution)/shard_map/all_to_all | solution.py:96

commit v2 on v1

--- a/solution.py
+++ b/solution.py
@@ -1,6 +1,10 @@
+import functools
+
 import jax
 import jax.numpy as jnp
 from jax import lax
+from jax.experimental import pallas as pl
+from jax.experimental.pallas import tpu as pltpu
 from jax.sharding import PartitionSpec as P
 
 S = 64
@@ -111,6 +115,71 @@
     return jnp.stack([high, value - high], axis=1).astype(BF16)
 
 
+def band_kernel(rows, width, x_ref, cot_ref, wc_ref, wct_ref, wd_ref, wdt_ref, pooled_ref, grad_ref, cg_ref, dg_ref, gpad_ref):
+    tiles = x_ref.shape[0]
+    span = rows * width
+    half = (width - 2) // 2
+    offs = [i * width + j for i in range(3) for j in range(3)]
+    m = lax.broadcasted_iota(jnp.int32, (span, pooled_ref.shape[2]), 0)
+    n = lax.broadcasted_iota(jnp.int32, (span, pooled_ref.shape[2]), 1)
+    sels = []
+    for p in range(2):
+        for q in range(2):
+            target = (2 * (n // half) + p) * width + 2 * (n % half) + q
+            sels.append(jnp.where(m == target, 1.0, 0.0).astype(BF16))
+    cout, cin, lanes = wc_ref.shape[1], wc_ref.shape[2], x_ref.shape[2]
+    cg = [jnp.zeros((cout, cin), F32) for _ in range(9)]
+    dg = [jnp.zeros((cout, cout), F32) for _ in range(4)]
+    nt = (((1,), (1,)), ((), ()))
+    gpad_ref[...] = jnp.zeros(gpad_ref.shape, gpad_ref.dtype)
+    for t in range(tiles):
+        xs = [x_ref[t, :, o:o + span] for o in offs]
+        pre = jnp.zeros((cout, span), F32)
+        for k in range(9):
+            pre = pre + jnp.dot(wc_ref[k], xs[k], preferred_element_type=F32)
+        gate = jax.nn.sigmoid(pre)
+        act = (pre * gate).astype(BF16)
+        cot = cot_ref[t]
+        pooled = jnp.zeros(pooled_ref.shape[1:], F32)
+        gact = jnp.zeros((cout, span), F32)
+        for k in range(4):
+            picked = jnp.dot(act, sels[k], preferred_element_type=F32).astype(BF16)
+            pooled = pooled + jnp.dot(wd_ref[k], picked, preferred_element_type=F32)
+            dg[k] = dg[k] + lax.dot_general(cot, picked, nt, preferred_element_type=F32)
+            spread = lax.dot_general(cot, sels[k], nt, preferred_element_type=F32).astype(BF16)
+            gact = gact + jnp.dot(wdt_ref[k], spread, preferred_element_type=F32)
+        pooled_ref[t] = pooled.astype(BF16)
+        gpre = (gact * (gate * (1.0 + pre * (1.0 - gate)))).astype(BF16)
+        for k in range(9):
+            cg[k] = cg[k] + lax.dot_general(gpre, xs[k], nt, preferred_element_type=F32)
+        gpad_ref[:, 256:256 + span] = gpre
+        total = jnp.zeros((cin, lanes), F32)
+        for k in range(9):
+            total = total + jnp.dot(wct_ref[k], gpad_ref[:, 256 - offs[k]:256 - offs[k] + lanes], preferred_element_type=F32)
+        grad_ref[t] = total.astype(grad_ref.dtype)
+    for k in range(9):
+        cg_ref[k] = cg[k]
+    for k in range(4):
+        dg_ref[k] = dg[k]
+
+def band_call(rows, width, x, cot, wc, wct, wd, wdt):
+    tiles, cin, lanes = x.shape
+    cout = wc.shape[1]
+    vm = pl.BlockSpec(memory_space=pltpu.VMEM)
+    return pl.pallas_call(
+        functools.partial(band_kernel, rows, width),
+        out_shape=(
+            jax.ShapeDtypeStruct((tiles, cout, cot.shape[2]), BF16),
+            jax.ShapeDtypeStruct((tiles, cin, lanes), BF16),
+            jax.ShapeDtypeStruct((9, cout, cin), F32),
+            jax.ShapeDtypeStruct((4, cout, cout), F32),
+        ),
+        in_specs=[vm] * 6,
+        out_specs=(vm, vm, vm, vm),
+        scratch_shapes=[pltpu.VMEM((cout, lanes + 256), BF16)],
+    )(x, cot, wc, wct, wd, wdt)
+
+
 def shards(features, conv_weight, down_weight, cotangent, partner, orientation):
     tiles, share, _ = features.shape
     n_chan = lax.axis_size("chan")
@@ -136,47 +205,27 @@
     bands = jnp.stack([padded[:, :, rows * b : rows * b + rows + 2, :] for b in range(n_chan)])
     cot_bands = jnp.moveaxis(cotangent.reshape(tiles, out_share, n_chan, rows // 2 * half), 2, 0)
     band_in, cot_in, w_in = exchange([bands, cot_bands, to_all(weights, n_chan)], "chan")
-    block = jnp.moveaxis(band_in, 0, 1).reshape(tiles, in_channels, rows + 2, S + 2)
-    grad_band = jnp.moveaxis(cot_in, 0, 1).reshape(tiles, out_channels, rows // 2, half)
+    width = S + 2
+    grid = (rows + 2) * width
+    lanes = -(-(grid + 2 * width + 2) // 128) * 128
+    block = jnp.moveaxis(band_in, 0, 1).reshape(tiles, in_channels, grid)
+    block = jnp.pad(block, ((0, 0), (0, 0), (0, lanes - grid)))
+    grad_band = jnp.moveaxis(cot_in, 0, 1).reshape(tiles, out_channels, rows // 2 * half)
     w_full = w_in.reshape(out_channels, conv_cols + down_cols)
     conv_full = w_full[:, :conv_cols].reshape(out_channels, 9, in_channels)
     down_full = w_full[:, conv_cols:].reshape(out_channels, 4, out_channels)
-
-    plain = ("NCHW", "OIHW", "NCHW")
-    swapped = ("CNHW", "IOHW", "NCHW")
-    w_conv = conv_full.reshape(out_channels, 3, 3, in_channels).transpose(0, 3, 1, 2)
-    w_down = down_full.reshape(out_channels, 2, 2, out_channels).transpose(0, 3, 1, 2)
-    pre_act = lax.conv_general_dilated(
-        block, w_conv, (1, 1), "VALID", dimension_numbers=plain, preferred_element_type=F32
-    )
-    activated = jax.nn.silu(pre_act).astype(BF16)
-    pooled_rows = lax.conv_general_dilated(
-        activated, w_down, (2, 2), "VALID", dimension_numbers=plain, preferred_element_type=F32
-    ).astype(BF16)
-    down_part = lax.conv_general_dilated(
-        activated, grad_band, (1, 1), "VALID", rhs_dilation=(2, 2),
-        dimension_numbers=swapped, preferred_element_type=F32,
-    )
-    down_part = down_part.transpose(1, 2, 3, 0).reshape(out_channels, down_cols)
-    w_up = jnp.flip(w_down, (2, 3)).transpose(1, 0, 2, 3)
-    grad_act = lax.conv_general_dilated(
-        grad_band, w_up, (1, 1), ((1, 1), (1, 1)), lhs_dilation=(2, 2),
-        dimension_numbers=plain, preferred_element_type=F32,
-    )
-    grad_pre = (grad_act * silu_grad(pre_act)).astype(BF16)
-    conv_part = lax.conv_general_dilated(
-        block, grad_pre, (1, 1), "VALID", dimension_numbers=swapped, preferred_element_type=F32
-    )
-    conv_part = conv_part.transpose(1, 2, 3, 0).reshape(out_channels, conv_cols)
-    w_back_conv = jnp.flip(w_conv, (2, 3)).transpose(1, 0, 2, 3)
-    grad_block = lax.conv_general_dilated(
-        grad_pre, w_back_conv, (1, 1), ((2, 2), (2, 2)), dimension_numbers=plain,
-        preferred_element_type=F32,
-    )
+    pooled_rows, grad_flat, conv_taps, down_taps = band_call(
+        rows, width, block, grad_band,
+        conv_full.transpose(1, 0, 2), conv_full.transpose(1, 2, 0),
+        down_full.transpose(1, 0, 2), down_full.transpose(1, 2, 0),
+    )
+    conv_part = conv_taps.transpose(1, 0, 2).reshape(out_channels, conv_cols)
+    down_part = down_taps.transpose(1, 0, 2).reshape(out_channels, down_cols)
+    grad_block = grad_flat[:, :, :grid].reshape(tiles, in_channels, rows + 2, width)
 
     pooled_out = jnp.moveaxis(pooled_rows.reshape(tiles, n_chan, out_share, rows // 2 * half), 1, 0)
     grad_out = jnp.moveaxis(
-        grad_block.astype(BF16).reshape(tiles, n_chan, share, rows + 2, S + 2), 1, 0
+        grad_block.reshape(tiles, n_chan, share, rows + 2, S + 2), 1, 0
     )
     w_part = jnp.concatenate([conv_part, down_part], axis=1)
     w_part = split_wide(w_part.reshape(n_chan, out_share * (conv_cols + down_cols)))

time: 162 us -> 167 us (1.031)
  Pallas kernels: 0 us -> 8.29 us
  matrix products: 4.61 us -> 0 us
  local copies, waits for them, and re-layouts: 31.7 us -> 34.5 us
    pallas_call x0 -> x1, Pallas kernels: none -> 8.29 us  [band_call(): pl.pallas_call(functools.partial(band_kernel, rows, width), out_shape=(ja...]
    transpose x4 -> x7, local copies, waits for them, and re-layouts: 0.34 us -> 3.69 us  [the longest x1 1.08 us: shards(): down_part = down_taps.transpose(1, 0, 2).reshape(out_channels, down_cols)]
    transpose x2 -> x0, matrix products: 2.41 us -> none  [the longest x1 1.79 us: shards(): conv_part = conv_part.transpose(1, 2, 3, 0).reshape(out_channels, conv_cols)]
    conv_general_dilated x4 -> x0, matrix products: 2.2 us -> none  [the longest x1 1.01 us: shards(): lax.conv_general_dilated(grad_pre, w_back_conv, (1, 1), ((2, 2), (2, 2)),...]
    unnamed x32 -> x30, local copies, waits for them, and re-layouts: 7.83 us -> 6.92 us
where the time goes in v2:
time: 167 us
  blocking collectives  53.1 us (32%)
  waiting for transfers between devices  42.3 us (25%)
  local copies, waits for them, and re-layouts  34.5 us (21%)
  starting transfers between devices  24.8 us (15%)
  Pallas kernels  8.29 us (5%)
  other arithmetic  2.43 us (1%)
    all_to_all x2, blocking collectives, exchange(): lax.all_to_all(buf.reshape(count, lanes // 128, 128), axis, 0, 0, tiled=T...  53.1 us
    all_to_all x3, waiting for transfers between devices, exchange(): lax.all_to_all(buf.reshape(count, lanes // 128, 128), axis, 0, 0, tiled=T...  42.3 us
    all_to_all x3, starting transfers between devices, exchange(): lax.all_to_all(buf.reshape(count, lanes // 128, 128), axis, 0, 0, tiled=T...  24.8 us
    pallas_call x1, Pallas kernels, band_call(): pl.pallas_call(functools.partial(band_kernel, rows, width), out_shape=(ja...  8.29 us
    unnamed x30, local copies, waits for them, and re-layouts  6.92 us
  transfers between devices with their start and end apart: 3, of which 3 were waited for; matrix products, arithmetic and copies ran while one was open for 3% of the time, Pallas kernels for 0%

profile of v2, /device:TPU:1, one launch (start us, length us, event | category | flops | bytes accessed | tf_op | source)
XLA Modules:
  0.0 166.9 jit_solution(4744842091068310970)
XLA Ops:
  0.6 1.2 reshape.243
  1.8 0.5 slice_reduce_fusion.1
  2.5 0.9 broadcast_in_dim.54
  3.4 11.6 %all-to-all-start = ((bf16[64,32,128]{2,1,0:T(8,128)(2,1)}), bf16[64,32,128]{2,1,0:T(8,128)(2,1)S(1)}, u32[]{:S(2)}, u32[]{:S(2)}) async-start(bf16[64,32,128]{2,1,0:T(8,128)(2,1)} %broadcast_in_dim.54), calls=%async_computation | async-start | bytes 1048576 | tf_op jit(solution)/shard_map/all_to_all | solution.py:100
  15.5 16.8 %all-to-all-done = bf16[64,32,128]{2,1,0:T(8,128)(2,1)S(1)} async-done(((bf16[64,32,128]{2,1,0:T(8,128)(2,1)}), bf16[64,32,128]{2,1,0:T(8,128)(2,1)S(1)}, u32[]{:S(2)}, u32[]{:S(2)}) %all-to-all-start) | async-done | bytes 524320 | tf_op jit(solution)/shard_map/all_to_all | solution.py:100
  32.3 0.4 reshape_reshape_reshape_reshape.3
  32.7 0.6 gather_fusion
  33.5 0.2 copy.344
  33.8 0.2 copy.343
  34.0 0.3 pad_maximum_fusion.2
  34.3 0.3 fusion.3
  34.5 0.2 stack.61
  34.7 0.2 stack.54
  35.0 0.2 stack.60
  35.2 0.2 stack.59
  35.4 0.2 stack.58
  36.1 1.6 stack.62
  37.7 0.4 concatenate.49
  38.2 27.6 %all_to_all.25 = bf16[8,251,128]{2,1,0:T(8,128)(2,1)S(1)} all-to-all(bf16[8,251,128]{2,1,0:T(8,128)(2,1)S(1)} %copy.347), channel_id=1, replica_groups=mesh['space'=64,'chan'=8] {'chan'}, dimensions={0} | all-to-all | bytes 1028096 | tf_op jit(solution)/shard_map/all_to_all | solution.py:100
  65.8 0.3 copy.396
  66.4 0.3 reshape_reshape.10
  66.8 0.6 copy.349
  67.8 0.8 copy.353.wd_ref
  68.5 0.9 copy.352.wc_ref
  69.4 0.6 reshape.252
  70.1 0.3 reshape.253
  70.5 0.7 pad.33.x_ref
  71.2 8.3 %shard_map.93 = (bf16[2,128,128]{2,1,0:T(8,128)(2,1)}, bf16[2,64,896]{2,1,0:T(8,128)(2,1)}, f32[9,128,64]{2,1,0:T(8,128)}, f32[4,128,128]{2,1,0:T(8,128)}) custom-call(bf16[2,64,896]{2,1,0:T(8,128)(2,1)} %pad.33.x_ref, bf16[2,128,128]{2,1,0:T(8,128)(2,1)} %bitcast.145, bf16[9,128,64]{2,1,0:T(8,128)(2,1)} %copy.352.wc_ref, bf16[9,64,128]{2,1,0:T(8,128)(2,1)} %bitcast.131, ...), custom_call_target="tpu_custom_call" | custom-call | tf_op jit(solution)/shard_map/pallas_call | solution.py:169
  79.5 0.9 copy.354
  80.4 0.9 slice.153
  81.3 1.1 copy.357
  82.4 0.2 copy.356
  82.7 0.2 copy.358
  82.9 0.2 reshape.263
  83.2 0.6 reshape_reshape.11
  83.9 0.4 reshape.260
  84.4 1.3 dynamic-update-slice.1
  85.7 3.9 %dynamic-update-slice.2 = bf16[8,49536]{1,0:T(8,128)(2,1)S(1)} dynamic-update-slice(bf16[8,49536]{1,0:T(8,128)(2,1)S(1)} %dynamic-update-slice.1, bf16[8,34816]{1,0:T(8,128)(2,1)S(1)} %bitcast.122, s32[]{} %constant.51, s32[]{} %constant.53) | dynamic-update-slice | bytes 1114116
  89.7 0.2 dynamic-update-slice.3
  90.0 25.5 %all_to_all.26 = bf16[8,387,128]{2,1,0:T(8,128)(2,1)S(1)} all-to-all(bf16[8,387,128]{2,1,0:T(8,128)(2,1)S(1)} %copy.359), channel_id=1, replica_groups=mesh['space'=64,'chan'=8] {'chan'}, dimensions={0} | all-to-all | bytes 1585152 | tf_op jit(solution)/shard_map/all_to_all | solution.py:100
  115.7 0.4 convert_reduce_fusion
  116.1 0.5 reshape.276
  116.7 0.3 copy.361
  117.1 0.3 copy.363
  117.4 0.2 fusion.5
  118.5 0.3 copy.374
  118.8 0.3 copy.365
  119.3 0.2 concatenate.52
  119.5 1.2 reshape.271
  120.7 7.0 %all-to-all-start.3 = ((bf16[64,37,128]{2,1,0:T(8,128)(2,1)}), bf16[64,37,128]{2,1,0:T(8,128)(2,1)S(1)}, u32[]{:S(2)}, u32[]{:S(2)}) async-start(bf16[64,37,128]{2,1,0:T(8,128)(2,1)} %reshape.271), calls=%async_computation.3 | async-start | bytes 1310720 | tf_op jit(solution)/shard_map/all_to_all | solution.py:100
  127.7 0.7 reshape.267
  128.4 19.4 %all-to-all-done.3 = bf16[64,37,128]{2,1,0:T(8,128)(2,1)S(1)} async-done(((bf16[64,37,128]{2,1,0:T(8,128)(2,1)}), bf16[64,37,128]{2,1,0:T(8,128)(2,1)S(1)}, u32[]{:S(2)}, u32[]{:S(2)}) %all-to-all-start.3) | async-done | bytes 606240 | tf_op jit(solution)/shard_map/all_to_all | solution.py:100
  148.1 0.7 concatenate.55
  148.7 6.3 %all-to-all-start.4 = ((f32[64,3,128]{2,1,0:T(4,128)}), f32[64,3,128]{2,1,0:T(4,128)S(1)}, u32[]{:S(2)}, u32[]{:S(2)}) async-start(f32[64,3,128]{2,1,0:T(4,128)} %concatenate.55), calls=%async_computation.4 | async-start | bytes 262144 | tf_op jit(solution)/shard_map/all_to_all | solution.py:100
  155.0 1.1 reshape_reshape_reshape.3
  156.1 0.6 gather_fusion.1
  157.0 0.3 copy.368
  157.3 0.3 copy.369
  157.6 0.4 fusion.1
  158.0 0.3 copy.370
  158.2 0.9 reshape.274
  159.2 6.1 %all-to-all-done.4 = f32[64,3,128]{2,1,0:T(4,128)S(1)} async-done(((f32[64,3,128]{2,1,0:T(4,128)}), f32[64,3,128]{2,1,0:T(4,128)S(1)}, u32[]{:S(2)}, u32[]{:S(2)}) %all-to-all-start.4) | async-done | bytes 98336 | tf_op jit(solution)/shard_map/all_to_all | solution.py:100
  165.5 0.6 mul.23
  166.2 0.7 copy.371
  (95 shorter events, 4.7 us)
Async XLA Ops:
  1.8 13.2 %copy-start.6 = (s32[2,4]{1,0:T(2,128)S(1)}, s32[2,4]{1,0:T(2,128)}, u32[]{:S(2)}) copy-start(s32[2,4]{1,0:T(2,128)} %param.12) | copy-start | bytes 100
  1.8 13.2 %copy-start.5 = (bf16[16,4,128]{2,1,0:T(4,128)(2,1)S(1)}, bf16[16,4,128]{2,1,0:T(4,128)(2,1)}, u32[]{:S(2)}) copy-start(bf16[16,4,128]{2,1,0:T(4,128)(2,1)} %param.10) | copy-start | bytes 49156
  1.8 13.2 %copy-start.4 = (bf16[16,9,64]{2,0,1:T(8,128)(2,1)S(1)}, bf16[16,9,64]{2,0,1:T(8,128)(2,1)}, u32[]{:S(2)}) copy-start(bf16[16,9,64]{2,0,1:T(8,128)(2,1)} %param.9) | copy-start | bytes 55300
  2.4 13.1 %copy-start.3 = (bf16[2,16,1024]{2,1,0:T(8,128)(2,1)S(1)}, bf16[2,16,1024]{2,1,0:T(8,128)(2,1)}, u32[]{:S(2)}) copy-start(bf16[2,16,1024]{2,1,0:T(8,128)(2,1)} %param.11) | copy-start | bytes 196612
  2.5 13.0 %copy-start.7 = (s32[2,4]{1,0:T(2,128)S(1)}, s32[2,4]{1,0:T(2,128)}, u32[]{:S(2)}) copy-start(s32[2,4]{1,0:T(2,128)} %param.13) | copy-start | bytes 100
  3.4 28.9 %all-to-all-start = ((bf16[64,32,128]{2,1,0:T(8,128)(2,1)}), bf16[64,32,128]{2,1,0:T(8,128)(2,1)S(1)}, u32[]{:S(2)}, u32[]{:S(2)}) async-start(bf16[64,32,128]{2,1,0:T(8,128)(2,1)} %broadcast_in_dim.54), calls=%async_computation | async-start | bytes 1048576 | tf_op jit(solution)/shard_map/all_to_all | solution.py:100
  67.6 2.5 %copy-start = (bf16[128,576]{0,1:T(8,128)(2,1)}, bf16[128,576]{0,1:T(8,128)(2,1)S(1)}, u32[]{:S(2)}) copy-start(bf16[128,576]{0,1:T(8,128)(2,1)S(1)} %copy.350) | copy-start | bytes 442372
  67.7 2.3 %copy-start.1 = (bf16[128,512]{0,1:T(8,128)(2,1)}, bf16[128,512]{0,1:T(8,128)(2,1)S(1)}, u32[]{:S(2)}) copy-start(bf16[128,512]{0,1:T(8,128)(2,1)S(1)} %copy.351) | copy-start | bytes 393220
  79.5 2.9 %copy-start.2 = (f32[9,128,64]{2,1,0:T(8,128)S(1)}, f32[9,128,64]{2,1,0:T(8,128)}, u32[]{:S(2)}) copy-start(f32[9,128,64]{2,1,0:T(8,128)} %get-tuple-element.11) | copy-start | bytes 884740
  120.7 27.1 %all-to-all-start.3 = ((bf16[64,37,128]{2,1,0:T(8,128)(2,1)}), bf16[64,37,128]{2,1,0:T(8,128)(2,1)S(1)}, u32[]{:S(2)}, u32[]{:S(2)}) async-start(bf16[64,37,128]{2,1,0:T(8,128)(2,1)} %reshape.271), calls=%async_computation.3 | async-start | bytes 1310720 | tf_op jit(solution)/shard_map/all_to_all | solution.py:100
  148.7 16.6 %all-to-all-start.4 = ((f32[64,3,128]{2,1,0:T(4,128)}), f32[64,3,128]{2,1,0:T(4,128)S(1)}, u32[]{:S(2)}, u32[]{:S(2)}) async-start(f32[64,3,128]{2,1,0:T(4,128)} %concatenate.55), calls=%async_computation.4 | async-start | bytes 262144 | tf_op jit(solution)/shard_map/all_to_all | solution.py:100

commit v3 on v1

--- a/solution.py
+++ b/solution.py
@@ -88,17 +88,19 @@
 
 def exchange(parts, axis):
     count = parts[0].shape[0]
-    flat = [p.reshape(count, -1) for p in parts]
-    sizes = [f.shape[1] for f in flat]
-    total = sum(sizes)
-    lanes = -(-total // 128) * 128
-    buf = jnp.concatenate(flat + [jnp.zeros((count, lanes - total), flat[0].dtype)], axis=1)
-    got = lax.all_to_all(buf.reshape(count, lanes // 128, 128), axis, 0, 0, tiled=True)
-    got = got.reshape(count, lanes)
+    tile = 4096 // parts[0].dtype.itemsize
+    flat = []
+    for i, p in enumerate(parts):
+        size = p[0].size
+        step = 128 if i == len(parts) - 1 else tile
+        padded = jnp.pad(p.reshape(count, size), ((0, 0), (0, -size % step)))
+        flat.append(padded.reshape(count, -1, 128))
+    got = lax.all_to_all(jnp.concatenate(flat, axis=1), axis, 0, 0, tiled=True)
     out, start = [], 0
-    for p, size in zip(parts, sizes):
-        out.append(got[:, start : start + size].reshape(p.shape))
-        start += size
+    for p, f in zip(parts, flat):
+        piece = got[:, start : start + f.shape[1]].reshape(count, -1)
+        out.append(piece[:, : p[0].size].reshape(p.shape))
+        start += f.shape[1]
     return out
 
 
@@ -135,7 +137,7 @@
 
     bands = jnp.stack([padded[:, :, rows * b : rows * b + rows + 2, :] for b in range(n_chan)])
     cot_bands = jnp.moveaxis(cotangent.reshape(tiles, out_share, n_chan, rows // 2 * half), 2, 0)
-    band_in, cot_in, w_in = exchange([bands, cot_bands, to_all(weights, n_chan)], "chan")
+    cot_in, w_in, band_in = exchange([cot_bands, to_all(weights, n_chan), bands], "chan")
     block = jnp.moveaxis(band_in, 0, 1).reshape(tiles, in_channels, rows + 2, S + 2)
     grad_band = jnp.moveaxis(cot_in, 0, 1).reshape(tiles, out_channels, rows // 2, half)
     w_full = w_in.reshape(out_channels, conv_cols + down_cols)
@@ -180,7 +182,7 @@
     )
     w_part = jnp.concatenate([conv_part, down_part], axis=1)
     w_part = split_wide(w_part.reshape(n_chan, out_share * (conv_cols + down_cols)))
-    pooled_in, grad_in, w_back = exchange([pooled_out, grad_out, w_part], "chan")
+    pooled_in, w_back, grad_in = exchange([pooled_out, w_part, grad_out], "chan")
     pooled = jnp.moveaxis(pooled_in, 0, 2).reshape(tiles, out_share, half * half)
     w_sum = jnp.sum(w_back.astype(F32), axis=(0, 1))
 

time: 162 us -> 156 us (0.963)
  local copies, waits for them, and re-layouts: 31.7 us -> 24.2 us
    unnamed x32 -> x30, local copies, waits for them, and re-layouts: 7.83 us -> 2.17 us
where the time goes in v3:
time: 156 us
  blocking collectives  53.3 us (34%)
  waiting for transfers between devices  43 us (28%)
  starting transfers between devices  25 us (16%)
  local copies, waits for them, and re-layouts  24.2 us (16%)
  matrix products  4.63 us (3%)
  other arithmetic  4.07 us (3%)
  between operations  1.7 us (1%)
    all_to_all x2, blocking collectives, exchange(): got = lax.all_to_all(jnp.concatenate(flat, axis=1), axis, 0, 0, tiled=True)  53.3 us
    all_to_all x3, waiting for transfers between devices, exchange(): got = lax.all_to_all(jnp.concatenate(flat, axis=1), axis, 0, 0, tiled=True)  43 us
    all_to_all x3, starting transfers between devices, exchange(): got = lax.all_to_all(jnp.concatenate(flat, axis=1), axis, 0, 0, tiled=True)  25 us
  transfers between devices with their start and end apart: 3, of which 3 were waited for; matrix products, arithmetic and copies ran while one was open for 3% of the time, Pallas kernels for 0%

profile of v3, /device:TPU:1, one launch (start us, length us, event | category | flops | bytes accessed | tf_op | source)
XLA Modules:
  0.0 155.9 jit_solution(12255854278480735396)
XLA Ops:
  0.6 1.2 reshape.256
  1.9 0.5 slice_reduce_fusion.1
  2.5 0.9 broadcast_in_dim.49
  3.4 11.6 %all-to-all-start = ((bf16[64,32,128]{2,1,0:T(8,128)(2,1)}), bf16[64,32,128]{2,1,0:T(8,128)(2,1)S(1)}, u32[]{:S(2)}, u32[]{:S(2)}) async-start(bf16[64,32,128]{2,1,0:T(8,128)(2,1)} %broadcast_in_dim.49), calls=%async_computation | async-start | bytes 1048576 | tf_op jit(solution)/shard_map/all_to_all | solution.py:98
  15.6 16.7 %all-to-all-done = bf16[64,32,128]{2,1,0:T(8,128)(2,1)S(1)} async-done(((bf16[64,32,128]{2,1,0:T(8,128)(2,1)}), bf16[64,32,128]{2,1,0:T(8,128)(2,1)S(1)}, u32[]{:S(2)}, u32[]{:S(2)}) %all-to-all-start) | async-done | bytes 524320 | tf_op jit(solution)/shard_map/all_to_all | solution.py:98
  32.3 0.4 reshape_reshape_reshape_reshape.6
  32.7 0.6 gather_fusion
  33.6 0.2 copy.509
  33.8 0.2 copy.508
  34.0 0.3 pad_maximum_fusion.5
  34.3 0.3 fusion.25
  34.6 0.2 stack.61
  34.8 0.2 stack.54
  35.1 0.2 stack.60
  35.3 0.2 stack.59
  36.1 1.6 %stack.62 = bf16[8,10560]{1,0:T(8,128)(2,1)S(1)} concatenate(bf16[1,10560]{1,0:T(2,128)(2,1)S(1)} %stack.54, bf16[1,10560]{1,0:T(2,128)(2,1)S(1)} %stack.55, bf16[1,10560]{1,0:T(2,128)(2,1)S(1)} %stack.56, bf16[1,10560]{1,0:T(2,128)(2,1)S(1)} %stack.57, bf16[1,10560]{1,0:T(2,128)(2,1)S(1)} %stack.58, bf16[1,10560]{1,0:T(2,128)(2,1)S(1)} %stack.59, bf16[1,10560]{1,0:T(2,128)(2,1)S(1)} %stack.60, ...), dimensions={0} | concatenate | bytes 337920 | tf_op jit(solution)/shard_map/stack | solution.py:138
  37.9 27.9 %all_to_all.25 = bf16[8,259,128]{2,1,0:T(8,128)(2,1)S(1)} all-to-all(bf16[8,259,128]{2,1,0:T(8,128)(2,1)S(1)} %pad_maximum_fusion.4), channel_id=1, replica_groups=mesh['space'=64,'chan'=8] {'chan'}, dimensions={0} | all-to-all | bytes 1060864 | tf_op jit(solution)/shard_map/all_to_all | solution.py:98
  66.0 0.3 reshape_reshape.19
  67.3 0.6 reshape.261
  67.9 0.4 copy.529
  68.4 0.4 copy.560
  68.8 0.4 pad.71.clone
  69.2 0.5 fusion.7
  69.7 0.3 convolution_select_fusion.1
  70.0 0.4 copy.527
  70.4 0.7 add_multiply_fusion
  71.1 0.2 copy.528
  71.3 1.8 %fusion.20 = f32[128,3,3,64]{0,3,2,1:T(8,128)S(1)} fusion(bf16[2,64,10,66]{1,0,3,2:T(2,128)(2,1)S(1)} %copy.529, bf16[8,2,64,128]{3,0,2,1:T(8,128)(2,1)S(1)} %fusion.6), kind=kOutput, calls=%fused_computation.54 | convolution fusion | flops 150994944 | bytes 726016 | tf_op jit(solution)/shard_map/transpose | solution.py:172
  73.4 0.4 copy-done.7
  73.8 1.0 fusion
  75.0 0.2 reshape.308
  75.3 0.2 copy.540
  75.5 0.2 copy.541
  75.8 0.4 reshape.271
  76.3 0.2 broadcast_select_fusion
  76.8 0.2 convolution_convert_fusion
  77.1 0.2 copy.522
  77.6 0.6 fusion.18
  78.5 0.2 reshape.269
  78.9 0.6 copy.536
  79.4 0.4 convert_element_type.76
  79.9 25.4 %all_to_all.26 = bf16[8,387,128]{2,1,0:T(8,128)(2,1)S(1)} all-to-all(bf16[8,387,128]{2,1,0:T(8,128)(2,1)S(1)} %pad_maximum_fusion), channel_id=1, replica_groups=mesh['space'=64,'chan'=8] {'chan'}, dimensions={0} | all-to-all | bytes 1585152 | tf_op jit(solution)/shard_map/all_to_all | solution.py:98
  105.3 0.5 reshape.315
  106.0 0.3 copy.545
  106.4 0.3 copy.547
  106.7 0.2 fusion.30
  108.0 0.3 copy.559
  108.3 0.3 copy.549
  108.8 0.9 pad_maximum_fusion.1
  109.7 7.1 %all-to-all-start.3 = ((bf16[64,37,128]{2,1,0:T(8,128)(2,1)}), bf16[64,37,128]{2,1,0:T(8,128)(2,1)S(1)}, u32[]{:S(2)}, u32[]{:S(2)}) async-start(bf16[64,37,128]{2,1,0:T(8,128)(2,1)} %pad_maximum_fusion.1), calls=%async_computation.3 | async-start | bytes 1310720 | tf_op jit(solution)/shard_map/all_to_all | solution.py:98
  116.8 0.6 copy.607
  117.4 19.4 %all-to-all-done.3 = bf16[64,37,128]{2,1,0:T(8,128)(2,1)S(1)} async-done(((bf16[64,37,128]{2,1,0:T(8,128)(2,1)}), bf16[64,37,128]{2,1,0:T(8,128)(2,1)S(1)}, u32[]{:S(2)}, u32[]{:S(2)}) %all-to-all-start.3) | async-done | bytes 606240 | tf_op jit(solution)/shard_map/all_to_all | solution.py:98
  137.0 0.7 pad.70
  137.7 6.3 %all-to-all-start.4 = ((f32[64,3,128]{2,1,0:T(4,128)}), f32[64,3,128]{2,1,0:T(4,128)S(1)}, u32[]{:S(2)}, u32[]{:S(2)}) async-start(f32[64,3,128]{2,1,0:T(4,128)} %pad.70), calls=%async_computation.4 | async-start | bytes 262144 | tf_op jit(solution)/shard_map/all_to_all | solution.py:98
  144.0 0.4 reshape_reshape_reshape_reshape.7
  144.4 0.6 gather_fusion.1
  145.3 0.3 copy.552
  145.6 0.3 copy.553
  145.9 0.3 fusion.5
  146.3 0.3 copy.554
  146.5 0.9 reshape.280
  147.5 6.8 %all-to-all-done.4 = f32[64,3,128]{2,1,0:T(4,128)S(1)} async-done(((f32[64,3,128]{2,1,0:T(4,128)}), f32[64,3,128]{2,1,0:T(4,128)S(1)}, u32[]{:S(2)}, u32[]{:S(2)}) %all-to-all-start.4) | async-done | bytes 98336 | tf_op jit(solution)/shard_map/all_to_all | solution.py:98
  154.5 0.6 mul.40
  155.2 0.7 copy.555
  (127 shorter events, 6.8 us)
Async XLA Ops:
  0.6 14.9 %copy-start = (bf16[2,16,1024]{2,1,0:T(8,128)(2,1)S(1)}, bf16[2,16,1024]{2,1,0:T(8,128)(2,1)}, u32[]{:S(2)}) copy-start(bf16[2,16,1024]{2,1,0:T(8,128)(2,1)} %param.11) | copy-start | bytes 196612
  1.9 13.2 %copy-start.5 = (s32[2,4]{1,0:T(2,128)S(1)}, s32[2,4]{1,0:T(2,128)}, u32[]{:S(2)}) copy-start(s32[2,4]{1,0:T(2,128)} %param.12) | copy-start | bytes 100
  1.9 13.2 %copy-start.2 = (bf16[16,4,128]{2,1,0:T(4,128)(2,1)S(1)}, bf16[16,4,128]{2,1,0:T(4,128)(2,1)}, u32[]{:S(2)}) copy-start(bf16[16,4,128]{2,1,0:T(4,128)(2,1)} %param.10) | copy-start | bytes 49156
  1.9 13.2 %copy-start.1 = (bf16[16,9,64]{2,0,1:T(8,128)(2,1)S(1)}, bf16[16,9,64]{2,0,1:T(8,128)(2,1)}, u32[]{:S(2)}) copy-start(bf16[16,9,64]{2,0,1:T(8,128)(2,1)} %param.9) | copy-start | bytes 55300
  2.4 13.1 %copy-start.6 = (s32[2,4]{1,0:T(2,128)S(1)}, s32[2,4]{1,0:T(2,128)}, u32[]{:S(2)}) copy-start(s32[2,4]{1,0:T(2,128)} %param.13) | copy-start | bytes 100
  3.4 28.9 %all-to-all-start = ((bf16[64,32,128]{2,1,0:T(8,128)(2,1)}), bf16[64,32,128]{2,1,0:T(8,128)(2,1)S(1)}, u32[]{:S(2)}, u32[]{:S(2)}) async-start(bf16[64,32,128]{2,1,0:T(8,128)(2,1)} %broadcast_in_dim.49), calls=%async_computation | async-start | bytes 1048576 | tf_op jit(solution)/shard_map/all_to_all | solution.py:98
  68.3 1.3 copy-start.4
  69.7 0.7 copy-start.3
  73.2 0.7 copy-start.7
  109.7 27.2 %all-to-all-start.3 = ((bf16[64,37,128]{2,1,0:T(8,128)(2,1)}), bf16[64,37,128]{2,1,0:T(8,128)(2,1)S(1)}, u32[]{:S(2)}, u32[]{:S(2)}) async-start(bf16[64,37,128]{2,1,0:T(8,128)(2,1)} %pad_maximum_fusion.1), calls=%async_computation.3 | async-start | bytes 1310720 | tf_op jit(solution)/shard_map/all_to_all | solution.py:98
  137.7 16.6 %all-to-all-start.4 = ((f32[64,3,128]{2,1,0:T(4,128)}), f32[64,3,128]{2,1,0:T(4,128)S(1)}, u32[]{:S(2)}, u32[]{:S(2)}) async-start(f32[64,3,128]{2,1,0:T(4,128)} %pad.70), calls=%async_computation.4 | async-start | bytes 262144 | tf_op jit(solution)/shard_map/all_to_all | solution.py:98

commit v4 on v3

--- a/solution.py
+++ b/solution.py
@@ -110,7 +110,13 @@
 
 def split_wide(value):
     high = lax.reduce_precision(value, exponent_bits=8, mantissa_bits=7)
-    return jnp.stack([high, value - high], axis=1).astype(BF16)
+    return jnp.concatenate([high, value - high], axis=-1).astype(BF16)
+
+
+def join_wide(value):
+    half = value.shape[-1] // 2
+    wide = value.astype(F32)
+    return wide[..., :half] + wide[..., half:]
 
 
 def shards(features, conv_weight, down_weight, cotangent, partner, orientation):
@@ -135,7 +141,10 @@
     halo = bordering(strips_all.reshape((n_space * tiles,) + strips.shape[1:]), partner, orientation)
     padded = pad_cat(images, halo)
 
-    bands = jnp.stack([padded[:, :, rows * b : rows * b + rows + 2, :] for b in range(n_chan)])
+    head = padded[:, :, : S, :].reshape(tiles, share, n_chan, rows, S + 2)
+    tail = jnp.pad(padded[:, :, rows:, :], ((0, 0), (0, 0), (0, rows - 2), (0, 0)))
+    tail = tail.reshape(tiles, share, n_chan, rows, S + 2)[:, :, :, :2, :]
+    bands = jnp.moveaxis(jnp.concatenate([head, tail], axis=3), 2, 0)
     cot_bands = jnp.moveaxis(cotangent.reshape(tiles, out_share, n_chan, rows // 2 * half), 2, 0)
     cot_in, w_in, band_in = exchange([cot_bands, to_all(weights, n_chan), bands], "chan")
     block = jnp.moveaxis(band_in, 0, 1).reshape(tiles, in_channels, rows + 2, S + 2)
@@ -184,7 +193,7 @@
     w_part = split_wide(w_part.reshape(n_chan, out_share * (conv_cols + down_cols)))
     pooled_in, w_back, grad_in = exchange([pooled_out, w_part, grad_out], "chan")
     pooled = jnp.moveaxis(pooled_in, 0, 2).reshape(tiles, out_share, half * half)
-    w_sum = jnp.sum(w_back.astype(F32), axis=(0, 1))
+    w_sum = jnp.sum(join_wide(w_back), axis=0)
 
     g = grad_in.astype(F32)
     main = jnp.moveaxis(g[:, :, :, :rows, :], 0, 2).reshape(tiles, share, S, S + 2)
@@ -199,7 +208,7 @@
     piece = -(-w_len // n_space)
     w_pieces = jnp.pad(w_sum, (0, piece * n_space - w_len)).reshape(n_space, piece)
     rims_all, w_got = exchange([to_all(rims.astype(BF16), n_space), split_wide(w_pieces)], "space")
-    w_mine = jnp.sum(w_got.astype(F32), axis=(0, 1))
+    w_mine = jnp.sum(join_wide(w_got), axis=0)
     (w_all,) = exchange([to_all(w_mine, n_space)], "space")
     w_total = w_all.reshape(-1)[:w_len].reshape(out_share, conv_cols + down_cols)
 

time: 156 us -> 153 us (0.981)
  local copies, waits for them, and re-layouts: 24.2 us -> 20.7 us
    another operation x12 -> x1, local copies, waits for them, and re-layouts: 3.63 us -> 0.01 us  [the longest x9 2.94 us: shards(): jnp.stack([padded[:, :, rows * b:rows * b + rows + 2, :] for b in range(n...]
where the time goes in v4:
time: 153 us
  blocking collectives  53.3 us (35%)
  waiting for transfers between devices  43 us (28%)
  starting transfers between devices  25 us (16%)
  local copies, waits for them, and re-layouts  20.7 us (14%)
  other arithmetic  4.65 us (3%)
  matrix products  4.63 us (3%)
  between operations  1.61 us (1%)
    all_to_all x2, blocking collectives, exchange(): got = lax.all_to_all(jnp.concatenate(flat, axis=1), axis, 0, 0, tiled=True)  53.3 us
    all_to_all x3, waiting for transfers between devices, exchange(): got = lax.all_to_all(jnp.concatenate(flat, axis=1), axis, 0, 0, tiled=True)  43 us
    all_to_all x3, starting transfers between devices, exchange(): got = lax.all_to_all(jnp.concatenate(flat, axis=1), axis, 0, 0, tiled=True)  25 us
  transfers between devices with their start and end apart: 3, of which 3 were waited for; matrix products, arithmetic and copies ran while one was open for 3% of the time, Pallas kernels for 0%

profile of v4, /device:TPU:1, one launch (start us, length us, event | category | flops | bytes accessed | tf_op | source)
XLA Modules:
  0.0 152.9 jit_solution(720269686105334044)
XLA Ops:
  0.6 1.2 reshape.199
  1.9 0.5 slice_reduce_fusion.1
  2.5 0.9 broadcast_in_dim.49
  3.4 11.6 %all-to-all-start = ((bf16[64,32,128]{2,1,0:T(8,128)(2,1)}), bf16[64,32,128]{2,1,0:T(8,128)(2,1)S(1)}, u32[]{:S(2)}, u32[]{:S(2)}) async-start(bf16[64,32,128]{2,1,0:T(8,128)(2,1)} %broadcast_in_dim.49), calls=%async_computation | async-start | bytes 1048576 | tf_op jit(solution)/shard_map/all_to_all | solution.py:98
  15.6 16.7 %all-to-all-done = bf16[64,32,128]{2,1,0:T(8,128)(2,1)S(1)} async-done(((bf16[64,32,128]{2,1,0:T(8,128)(2,1)}), bf16[64,32,128]{2,1,0:T(8,128)(2,1)S(1)}, u32[]{:S(2)}, u32[]{:S(2)}) %all-to-all-start) | async-done | bytes 524320 | tf_op jit(solution)/shard_map/all_to_all | solution.py:98
  32.3 0.4 reshape_reshape_reshape_reshape.6
  32.7 0.6 gather_fusion
  33.6 0.2 copy.353
  33.8 0.2 copy.352
  34.1 0.8 fusion.34
  35.1 0.4 reshape.204
  35.7 27.9 %all_to_all.25 = bf16[8,259,128]{2,1,0:T(8,128)(2,1)S(1)} all-to-all(bf16[8,259,128]{2,1,0:T(8,128)(2,1)S(1)} %pad_maximum_fusion.3), channel_id=1, replica_groups=mesh['space'=64,'chan'=8] {'chan'}, dimensions={0} | all-to-all | bytes 1060864 | tf_op jit(solution)/shard_map/all_to_all | solution.py:98
  63.8 0.3 reshape_reshape.18
  64.5 0.2 reshape.212
  64.7 0.2 copy.379
  65.1 0.6 reshape.207
  65.7 0.4 copy.375
  66.2 0.4 copy.405
  66.6 0.4 pad.76.clone
  67.0 0.5 fusion.14
  67.5 0.3 convolution_select_fusion.1
  67.8 0.4 copy.373
  68.2 0.7 add_multiply_fusion
  68.9 0.2 copy.374
  69.1 1.8 %fusion.35 = f32[128,3,3,64]{0,3,2,1:T(8,128)S(1)} fusion(bf16[2,64,10,66]{1,0,3,2:T(2,128)(2,1)S(1)} %copy.375, bf16[8,2,64,128]{3,0,2,1:T(8,128)(2,1)S(1)} %fusion.7), kind=kOutput, calls=%fused_computation.76 | convolution fusion | flops 150994944 | bytes 726016 | tf_op jit(solution)/shard_map/transpose | solution.py:181
  71.0 0.2 copy.380
  71.2 0.4 copy-done.7
  71.6 1.0 fusion
  72.8 0.2 reshape.254
  73.1 0.2 copy.385
  73.3 0.2 copy.386
  73.6 0.4 reshape.217
  74.1 0.2 broadcast_select_fusion
  74.6 0.2 convolution_convert_fusion
  74.9 0.2 copy.368
  75.1 0.2 reshape.210
  75.4 0.6 fusion.25
  76.1 0.2 pad_maximum_fusion.2
  76.3 0.3 reshape.215
  76.7 25.4 %all_to_all.26 = bf16[8,387,128]{2,1,0:T(8,128)(2,1)S(1)} all-to-all(bf16[8,387,128]{2,1,0:T(8,128)(2,1)S(1)} %pad_maximum_fusion), channel_id=1, replica_groups=mesh['space'=64,'chan'=8] {'chan'}, dimensions={0} | all-to-all | bytes 1585152 | tf_op jit(solution)/shard_map/all_to_all | solution.py:98
  102.2 0.5 reshape.261
  102.8 0.3 copy.390
  103.2 0.3 copy.392
  103.6 0.2 fusion.47
  104.1 0.4 copy.449
  104.4 0.2 fusion.4
  105.0 0.3 copy.404
  105.3 0.3 copy.394
  105.7 0.9 pad_maximum_fusion.1
  106.6 7.1 %all-to-all-start.3 = ((bf16[64,37,128]{2,1,0:T(8,128)(2,1)}), bf16[64,37,128]{2,1,0:T(8,128)(2,1)S(1)}, u32[]{:S(2)}, u32[]{:S(2)}) async-start(bf16[64,37,128]{2,1,0:T(8,128)(2,1)} %pad_maximum_fusion.1), calls=%async_computation.3 | async-start | bytes 1310720 | tf_op jit(solution)/shard_map/all_to_all | solution.py:98
  113.7 0.6 copy.457
  114.4 19.4 %all-to-all-done.3 = bf16[64,37,128]{2,1,0:T(8,128)(2,1)S(1)} async-done(((bf16[64,37,128]{2,1,0:T(8,128)(2,1)}), bf16[64,37,128]{2,1,0:T(8,128)(2,1)S(1)}, u32[]{:S(2)}, u32[]{:S(2)}) %all-to-all-start.3) | async-done | bytes 606240 | tf_op jit(solution)/shard_map/all_to_all | solution.py:98
  134.0 0.7 pad.75
  134.7 6.3 %all-to-all-start.4 = ((f32[64,3,128]{2,1,0:T(4,128)}), f32[64,3,128]{2,1,0:T(4,128)S(1)}, u32[]{:S(2)}, u32[]{:S(2)}) async-start(f32[64,3,128]{2,1,0:T(4,128)} %pad.75), calls=%async_computation.4 | async-start | bytes 262144 | tf_op jit(solution)/shard_map/all_to_all | solution.py:98
  141.0 0.4 reshape_reshape_reshape_reshape.7
  141.4 0.6 gather_fusion.1
  142.2 0.3 copy.396
  142.6 0.3 copy.397
  142.9 0.3 fusion.6
  143.2 0.3 copy.398
  143.5 0.9 reshape.226
  144.5 6.8 %all-to-all-done.4 = f32[64,3,128]{2,1,0:T(4,128)S(1)} async-done(((f32[64,3,128]{2,1,0:T(4,128)}), f32[64,3,128]{2,1,0:T(4,128)S(1)}, u32[]{:S(2)}, u32[]{:S(2)}) %all-to-all-start.4) | async-done | bytes 98336 | tf_op jit(solution)/shard_map/all_to_all | solution.py:98
  151.5 0.6 mul.40
  152.2 0.7 copy.399
  (112 shorter events, 4.9 us)
Async XLA Ops:
  0.6 14.9 %copy-start = (bf16[2,16,1024]{2,1,0:T(8,128)(2,1)S(1)}, bf16[2,16,1024]{2,1,0:T(8,128)(2,1)}, u32[]{:S(2)}) copy-start(bf16[2,16,1024]{2,1,0:T(8,128)(2,1)} %param.11) | copy-start | bytes 196612
  1.9 13.2 %copy-start.5 = (s32[2,4]{1,0:T(2,128)S(1)}, s32[2,4]{1,0:T(2,128)}, u32[]{:S(2)}) copy-start(s32[2,4]{1,0:T(2,128)} %param.12) | copy-start | bytes 100
  1.9 13.2 %copy-start.2 = (bf16[16,4,128]{2,1,0:T(4,128)(2,1)S(1)}, bf16[16,4,128]{2,1,0:T(4,128)(2,1)}, u32[]{:S(2)}) copy-start(bf16[16,4,128]{2,1,0:T(4,128)(2,1)} %param.10) | copy-start | bytes 49156
  1.9 13.2 %copy-start.1 = (bf16[16,9,64]{2,0,1:T(8,128)(2,1)S(1)}, bf16[16,9,64]{2,0,1:T(8,128)(2,1)}, u32[]{:S(2)}) copy-start(bf16[16,9,64]{2,0,1:T(8,128)(2,1)} %param.9) | copy-start | bytes 55300
  2.4 13.1 %copy-start.6 = (s32[2,4]{1,0:T(2,128)S(1)}, s32[2,4]{1,0:T(2,128)}, u32[]{:S(2)}) copy-start(s32[2,4]{1,0:T(2,128)} %param.13) | copy-start | bytes 100
  3.4 28.9 %all-to-all-start = ((bf16[64,32,128]{2,1,0:T(8,128)(2,1)}), bf16[64,32,128]{2,1,0:T(8,128)(2,1)S(1)}, u32[]{:S(2)}, u32[]{:S(2)}) async-start(bf16[64,32,128]{2,1,0:T(8,128)(2,1)} %broadcast_in_dim.49), calls=%async_computation | async-start | bytes 1048576 | tf_op jit(solution)/shard_map/all_to_all | solution.py:98
  66.2 1.3 copy-start.4
  67.5 0.7 copy-start.3
  70.9 0.7 copy-start.7
  106.6 27.2 %all-to-all-start.3 = ((bf16[64,37,128]{2,1,0:T(8,128)(2,1)}), bf16[64,37,128]{2,1,0:T(8,128)(2,1)S(1)}, u32[]{:S(2)}, u32[]{:S(2)}) async-start(bf16[64,37,128]{2,1,0:T(8,128)(2,1)} %pad_maximum_fusion.1), calls=%async_computation.3 | async-start | bytes 1310720 | tf_op jit(solution)/shard_map/all_to_all | solution.py:98
  134.7 16.6 %all-to-all-start.4 = ((f32[64,3,128]{2,1,0:T(4,128)}), f32[64,3,128]{2,1,0:T(4,128)S(1)}, u32[]{:S(2)}, u32[]{:S(2)}) async-start(f32[64,3,128]{2,1,0:T(4,128)} %pad.75), calls=%async_computation.4 | async-start | bytes 262144 | tf_op jit(solution)/shard_map/all_to_all | solution.py:98

commit v5 on v4

--- a/solution.py
+++ b/solution.py
@@ -196,14 +196,20 @@
     w_sum = jnp.sum(join_wide(w_back), axis=0)
 
     g = grad_in.astype(F32)
-    main = jnp.moveaxis(g[:, :, :, :rows, :], 0, 2).reshape(tiles, share, S, S + 2)
-    extra = jnp.pad(g[:, :, :, rows:, :], ((0, 0), (0, 0), (0, 0), (0, rows - 2), (0, 0)))
-    extra = jnp.moveaxis(extra, 0, 2).reshape(tiles, share, S, S + 2)
-    grad_padded = jnp.pad(main, ((0, 0), (0, 0), (0, 2), (0, 0))) + jnp.pad(
-        extra, ((0, 0), (0, 0), (rows, 0), (0, 0))
-    )[:, :, : S + 2, :]
-
-    rims = rim_strips(grad_padded)
+
+    def assemble(bands_of):
+        width = bands_of.shape[-1]
+        main = jnp.moveaxis(bands_of[:, :, :, :rows, :], 0, 2).reshape(tiles, share, S, width)
+        extra = jnp.pad(bands_of[:, :, :, rows:, :], ((0, 0), (0, 0), (0, 0), (0, rows - 2), (0, 0)))
+        extra = jnp.moveaxis(extra, 0, 2).reshape(tiles, share, S, width)
+        return jnp.pad(main, ((0, 0), (0, 0), (0, 2), (0, 0))) + jnp.pad(
+            extra, ((0, 0), (0, 0), (rows, 0), (0, 0))
+        )[:, :, : S + 2, :]
+
+    sides = assemble(jnp.concatenate([g[..., :1], g[..., -1:]], axis=-1))
+    rims = jnp.stack(
+        [g[0, :, :, 0, 1:-1], sides[:, :, 1:-1, 1], g[-1, :, :, -1, 1:-1], sides[:, :, 1:-1, 0]], axis=1
+    )
     w_len = w_sum.shape[0]
     piece = -(-w_len // n_space)
     w_pieces = jnp.pad(w_sum, (0, piece * n_space - w_len)).reshape(n_space, piece)
@@ -214,7 +220,7 @@
 
     returned = bordering(rims_all.reshape((n_space * tiles,) + rims.shape[1:]), partner, orientation)
     returned = returned.astype(F32)
-    features_grad = add_edges(grad_padded[:, :, 1:-1, 1:-1], returned).astype(BF16)
+    features_grad = add_edges(assemble(g)[:, :, 1:-1, 1:-1], returned).astype(BF16)
     features_grad = features_grad.reshape(tiles, share, S * S)
     grad_scale = float(n_space * tiles * S * S) ** (-0.5)
     conv_grad = w_total[:, :conv_cols].reshape(conv_weight.shape) * grad_scale

time: 153 us -> 161 us (1.052)
  local copies, waits for them, and re-layouts: 20.7 us -> 27.2 us
  other arithmetic: 4.65 us -> 6.98 us
    slice x3 -> x6, local copies, waits for them, and re-layouts: 0.46 us -> 2.35 us  [the longest x3 2.01 us: shards(): sides = assemble(jnp.concatenate([g[..., :1], g[..., -1:]], axis=-1))]
    unnamed x31 -> x48, local copies, waits for them, and re-layouts: 2.52 us -> 3.51 us
  transfers between devices with their start and end apart: 3 -> 3, of which waited for: 3 -> 3; matrix products, arithmetic and copies ran while one was open for 3% -> 4% of each run, Pallas kernels for 0% -> 0%
where the time goes in v5:
time: 161 us; the launch traced here: 160 us
  blocking collectives  53.3 us (33%)
  waiting for transfers between devices  41.5 us (26%)
  local copies, waits for them, and re-layouts  27.2 us (17%)
  starting transfers between devices  25 us (16%)
  other arithmetic  6.98 us (4%)
  matrix products  4.63 us (3%)
  between operations  1.7 us (1%)
    all_to_all x2, blocking collectives, exchange(): got = lax.all_to_all(jnp.concatenate(flat, axis=1), axis, 0, 0, tiled=True)  53.3 us
    all_to_all x3, waiting for transfers between devices, exchange(): got = lax.all_to_all(jnp.concatenate(flat, axis=1), axis, 0, 0, tiled=True)  41.5 us
    all_to_all x3, starting transfers between devices, exchange(): got = lax.all_to_all(jnp.concatenate(flat, axis=1), axis, 0, 0, tiled=True)  25 us
    unnamed x48, local copies, waits for them, and re-layouts  3.51 us
  transfers between devices with their start and end apart: 3, of which 3 were waited for; matrix products, arithmetic and copies ran while one was open for 4% of the time, Pallas kernels for 0%

profile of v5, /device:TPU:1, one launch (start us, length us, event | category | flops | bytes accessed | tf_op | source)
XLA Modules:
  0.0 160.3 jit_solution(9868574628217197450)
XLA Ops:
  0.6 1.2 reshape.205
  1.9 0.5 slice_reduce_fusion.1
  2.5 0.9 broadcast_in_dim.49
  3.4 11.6 %all-to-all-start = ((bf16[64,32,128]{2,1,0:T(8,128)(2,1)}), bf16[64,32,128]{2,1,0:T(8,128)(2,1)S(1)}, u32[]{:S(2)}, u32[]{:S(2)}) async-start(bf16[64,32,128]{2,1,0:T(8,128)(2,1)} %broadcast_in_dim.49), calls=%async_computation | async-start | bytes 1048576 | tf_op jit(solution)/shard_map/all_to_all | solution.py:98
  15.6 16.7 %all-to-all-done = bf16[64,32,128]{2,1,0:T(8,128)(2,1)S(1)} async-done(((bf16[64,32,128]{2,1,0:T(8,128)(2,1)}), bf16[64,32,128]{2,1,0:T(8,128)(2,1)S(1)}, u32[]{:S(2)}, u32[]{:S(2)}) %all-to-all-start) | async-done | bytes 524320 | tf_op jit(solution)/shard_map/all_to_all | solution.py:98
  32.3 0.4 reshape_reshape_reshape_reshape.6
  32.7 0.6 gather_fusion
  33.6 0.2 copy.358
  33.8 0.2 copy.357
  34.1 0.8 fusion.35
  35.1 0.4 reshape.210
  35.7 27.9 %all_to_all.25 = bf16[8,259,128]{2,1,0:T(8,128)(2,1)S(1)} all-to-all(bf16[8,259,128]{2,1,0:T(8,128)(2,1)S(1)} %pad_maximum_fusion.3), channel_id=1, replica_groups=mesh['space'=64,'chan'=8] {'chan'}, dimensions={0} | all-to-all | bytes 1060864 | tf_op jit(solution)/shard_map/all_to_all | solution.py:98
  63.8 0.3 reshape_reshape.18
  65.1 0.6 reshape.213
  65.8 0.4 copy.380
  66.2 0.4 copy.419
  66.6 0.4 pad.91.clone
  67.0 0.5 fusion.15
  67.5 0.3 convolution_select_fusion.1
  67.8 0.4 copy.378
  68.2 0.7 add_multiply_fusion
  69.2 1.8 %fusion.36 = f32[128,3,3,64]{0,3,2,1:T(8,128)S(1)} fusion(bf16[2,64,10,66]{1,0,3,2:T(2,128)(2,1)S(1)} %copy.380, bf16[8,2,64,128]{3,0,2,1:T(8,128)(2,1)S(1)} %fusion.8), kind=kOutput, calls=%fused_computation.77 | convolution fusion | flops 150994944 | bytes 726016 | tf_op jit(solution)/shard_map/transpose | solution.py:181
  71.3 0.4 copy-done.15
  71.7 1.0 fusion
  72.9 0.2 reshape.262
  73.1 0.2 copy.390
  73.4 0.2 copy.391
  73.6 0.4 reshape.223
  74.1 0.2 broadcast_select_fusion
  74.6 0.2 convolution_convert_fusion
  75.4 0.6 fusion.26
  76.3 0.3 reshape.221
  76.8 25.4 %all_to_all.26 = bf16[8,387,128]{2,1,0:T(8,128)(2,1)S(1)} all-to-all(bf16[8,387,128]{2,1,0:T(8,128)(2,1)S(1)} %pad_maximum_fusion), channel_id=1, replica_groups=mesh['space'=64,'chan'=8] {'chan'}, dimensions={0} | all-to-all | bytes 1585152 | tf_op jit(solution)/shard_map/all_to_all | solution.py:98
  102.2 0.6 convert_element_type.79
  102.9 0.3 fusion.50
  103.3 0.4 copy.465
  103.7 0.8 fusion.4
  104.5 1.6 %reshape.231 = f32[64,272]{1,0:T(8,128)} reshape(f32[17408]{0:T(1024)} %fusion.4) | data formatting | bytes 139264 | tf_op jit(solution)/shard_map/reshape | solution.py:215
  106.1 0.9 reduce-precision_convert_fusion.1
  107.0 0.7 fusion.44
  107.7 1.6 %reshape.232 = bf16[64,5,128]{2,1,0:T(8,128)(2,1)} reshape(bf16[64,640]{1,0:T(8,128)(2,1)} %fusion.44) | data formatting | bytes 163840 | tf_op jit(solution)/shard_map/reshape | solution.py:97
  109.4 0.6 copy.476
  110.0 0.6 copy.475
  110.6 0.9 copy.398
  111.4 0.9 copy.399
  113.2 0.9 pad_maximum_fusion.1
  114.1 7.1 %all-to-all-start.3 = ((bf16[64,37,128]{2,1,0:T(8,128)(2,1)}), bf16[64,37,128]{2,1,0:T(8,128)(2,1)S(1)}, u32[]{:S(2)}, u32[]{:S(2)}) async-start(bf16[64,37,128]{2,1,0:T(8,128)(2,1)} %pad_maximum_fusion.1), calls=%async_computation.3 | async-start | bytes 1310720 | tf_op jit(solution)/shard_map/all_to_all | solution.py:98
  121.4 0.6 copy.473
  122.1 0.3 copy.397
  122.5 0.3 copy.395
  122.8 0.2 pad_slice_fusion
  123.0 18.3 %all-to-all-done.3 = bf16[64,37,128]{2,1,0:T(8,128)(2,1)S(1)} async-done(((bf16[64,37,128]{2,1,0:T(8,128)(2,1)}), bf16[64,37,128]{2,1,0:T(8,128)(2,1)S(1)}, u32[]{:S(2)}, u32[]{:S(2)}) %all-to-all-start.3) | async-done | bytes 606240 | tf_op jit(solution)/shard_map/all_to_all | solution.py:98
  141.5 0.7 pad.90
  142.1 6.3 %all-to-all-start.4 = ((f32[64,3,128]{2,1,0:T(4,128)}), f32[64,3,128]{2,1,0:T(4,128)S(1)}, u32[]{:S(2)}, u32[]{:S(2)}) async-start(f32[64,3,128]{2,1,0:T(4,128)} %pad.90), calls=%async_computation.4 | async-start | bytes 262144 | tf_op jit(solution)/shard_map/all_to_all | solution.py:98
  148.5 0.4 reshape_reshape_reshape_reshape.7
  148.9 0.7 gather_fusion.1
  149.9 0.3 copy.405
  150.2 0.3 copy.406
  150.5 0.5 fusion.7
  151.0 0.3 copy.407
  151.3 0.9 reshape.234
  152.2 6.5 %all-to-all-done.4 = f32[64,3,128]{2,1,0:T(4,128)S(1)} async-done(((f32[64,3,128]{2,1,0:T(4,128)}), f32[64,3,128]{2,1,0:T(4,128)S(1)}, u32[]{:S(2)}, u32[]{:S(2)}) %all-to-all-start.4) | async-done | bytes 98336 | tf_op jit(solution)/shard_map/all_to_all | solution.py:98
  158.9 0.6 mul.40
  159.7 0.7 copy.408
  (137 shorter events, 6.4 us)
Async XLA Ops:
  0.6 14.9 %copy-start = (bf16[2,16,1024]{2,1,0:T(8,128)(2,1)S(1)}, bf16[2,16,1024]{2,1,0:T(8,128)(2,1)}, u32[]{:S(2)}) copy-start(bf16[2,16,1024]{2,1,0:T(8,128)(2,1)} %param.11) | copy-start | bytes 196612
  1.9 13.2 %copy-start.13 = (s32[2,4]{1,0:T(2,128)S(1)}, s32[2,4]{1,0:T(2,128)}, u32[]{:S(2)}) copy-start(s32[2,4]{1,0:T(2,128)} %param.12) | copy-start | bytes 100
  1.9 13.3 %copy-start.3 = (bf16[16,4,128]{2,1,0:T(4,128)(2,1)S(1)}, bf16[16,4,128]{2,1,0:T(4,128)(2,1)}, u32[]{:S(2)}) copy-start(bf16[16,4,128]{2,1,0:T(4,128)(2,1)} %param.10) | copy-start | bytes 49156
  1.9 13.3 %copy-start.2 = (bf16[16,9,64]{2,0,1:T(8,128)(2,1)S(1)}, bf16[16,9,64]{2,0,1:T(8,128)(2,1)}, u32[]{:S(2)}) copy-start(bf16[16,9,64]{2,0,1:T(8,128)(2,1)} %param.9) | copy-start | bytes 55300
  2.4 13.2 %copy-start.14 = (s32[2,4]{1,0:T(2,128)S(1)}, s32[2,4]{1,0:T(2,128)}, u32[]{:S(2)}) copy-start(s32[2,4]{1,0:T(2,128)} %param.13) | copy-start | bytes 100
  3.4 28.9 %all-to-all-start = ((bf16[64,32,128]{2,1,0:T(8,128)(2,1)}), bf16[64,32,128]{2,1,0:T(8,128)(2,1)S(1)}, u32[]{:S(2)}, u32[]{:S(2)}) async-start(bf16[64,32,128]{2,1,0:T(8,128)(2,1)} %broadcast_in_dim.49), calls=%async_computation | async-start | bytes 1048576 | tf_op jit(solution)/shard_map/all_to_all | solution.py:98
  15.5 18.3 %copy-start.6 = (s32[1024]{0:T(1024)}, s32[1024]{0:T(1024)S(1)}, u32[]{:S(2)}) copy-start(s32[1024]{0:T(1024)S(1)} %pad_clamp_fusion) | copy-start | bytes 12292
  15.6 18.5 %copy-start.11 = (pred[8]{0:T(512)(128)(4,1)}, pred[8]{0:T(512)(128)(4,1)S(1)}, u32[]{:S(2)}) copy-start(pred[8]{0:T(512)(128)(4,1)S(1)} %compare_and_fusion) | copy-start | bytes 28
  15.6 18.5 %copy-start.9 = (pred[2,4]{1,0:T(4,128)(4,1)}, pred[2,4]{1,0:T(4,128)(4,1)S(1)}, u32[]{:S(2)}) copy-start(pred[2,4]{1,0:T(4,128)(4,1)S(1)} %broadcast_compare_fusion) | copy-start | bytes 28
  66.2 1.3 copy-start.8
  67.5 0.7 copy-start.7
  71.0 0.7 copy-start.15
  111.4 1.5 copy-start.4
  111.4 1.5 copy-start.5
  112.3 0.9 copy-start.1
  114.1 27.2 %all-to-all-start.3 = ((bf16[64,37,128]{2,1,0:T(8,128)(2,1)}), bf16[64,37,128]{2,1,0:T(8,128)(2,1)S(1)}, u32[]{:S(2)}, u32[]{:S(2)}) async-start(bf16[64,37,128]{2,1,0:T(8,128)(2,1)} %pad_maximum_fusion.1), calls=%async_computation.3 | async-start | bytes 1310720 | tf_op jit(solution)/shard_map/all_to_all | solution.py:98
  142.1 16.6 %all-to-all-start.4 = ((f32[64,3,128]{2,1,0:T(4,128)}), f32[64,3,128]{2,1,0:T(4,128)S(1)}, u32[]{:S(2)}, u32[]{:S(2)}) async-start(f32[64,3,128]{2,1,0:T(4,128)} %pad.90), calls=%async_computation.4 | async-start | bytes 262144 | tf_op jit(solution)/shard_map/all_to_all | solution.py:98
  148.4 1.2 copy-start.12
  148.4 1.3 copy-start.10

commit v6 on v4

--- a/solution.py
+++ b/solution.py
@@ -189,8 +189,10 @@
     grad_out = jnp.moveaxis(
         grad_block.astype(BF16).reshape(tiles, n_chan, share, rows + 2, S + 2), 1, 0
     )
-    w_part = jnp.concatenate([conv_part, down_part], axis=1)
-    w_part = split_wide(w_part.reshape(n_chan, out_share * (conv_cols + down_cols)))
+    down_dest = down_part.reshape(n_chan, out_share * down_cols)
+    conv_dest = conv_part.reshape(n_chan, out_share, 9, in_channels).transpose(0, 2, 1, 3)
+    w_part = jnp.concatenate([down_dest, conv_dest.reshape(n_chan, out_share * conv_cols)], axis=1)
+    w_part = split_wide(w_part)
     pooled_in, w_back, grad_in = exchange([pooled_out, w_part, grad_out], "chan")
     pooled = jnp.moveaxis(pooled_in, 0, 2).reshape(tiles, out_share, half * half)
     w_sum = jnp.sum(join_wide(w_back), axis=0)
@@ -208,17 +210,18 @@
     piece = -(-w_len // n_space)
     w_pieces = jnp.pad(w_sum, (0, piece * n_space - w_len)).reshape(n_space, piece)
     rims_all, w_got = exchange([to_all(rims.astype(BF16), n_space), split_wide(w_pieces)], "space")
-    w_mine = jnp.sum(join_wide(w_got), axis=0)
+    grad_scale = float(n_space * tiles * S * S) ** (-0.5)
+    w_mine = jnp.sum(join_wide(w_got), axis=0) * grad_scale
     (w_all,) = exchange([to_all(w_mine, n_space)], "space")
-    w_total = w_all.reshape(-1)[:w_len].reshape(out_share, conv_cols + down_cols)
+    w_total = w_all.reshape(-1)[:w_len]
 
     returned = bordering(rims_all.reshape((n_space * tiles,) + rims.shape[1:]), partner, orientation)
     returned = returned.astype(F32)
     features_grad = add_edges(grad_padded[:, :, 1:-1, 1:-1], returned).astype(BF16)
     features_grad = features_grad.reshape(tiles, share, S * S)
-    grad_scale = float(n_space * tiles * S * S) ** (-0.5)
-    conv_grad = w_total[:, :conv_cols].reshape(conv_weight.shape) * grad_scale
-    down_grad = w_total[:, conv_cols:].reshape(down_weight.shape) * grad_scale
+    down_len = out_share * down_cols
+    down_grad = w_total[:down_len].reshape(down_weight.shape)
+    conv_grad = w_total[down_len:].reshape(9, out_share, in_channels).transpose(1, 0, 2)
     return (pooled, features_grad, conv_grad, down_grad)
 
 

time: 153 us -> 153 us (level)
  no operation moved by 1% of the time
where the time goes in v6:
time: 153 us
  blocking collectives  53.3 us (35%)
  waiting for transfers between devices  43 us (28%)
  starting transfers between devices  25 us (16%)
  local copies, waits for them, and re-layouts  20.8 us (14%)
  other arithmetic  4.51 us (3%)
  matrix products  4.5 us (3%)
  between operations  1.62 us (1%)
    all_to_all x2, blocking collectives, exchange(): got = lax.all_to_all(jnp.concatenate(flat, axis=1), axis, 0, 0, tiled=True)  53.3 us
    all_to_all x3, waiting for transfers between devices, exchange(): got = lax.all_to_all(jnp.concatenate(flat, axis=1), axis, 0, 0, tiled=True)  43 us
    all_to_all x3, starting transfers between devices, exchange(): got = lax.all_to_all(jnp.concatenate(flat, axis=1), axis, 0, 0, tiled=True)  25 us
  transfers between devices with their start and end apart: 3, of which 3 were waited for; matrix products, arithmetic and copies ran while one was open for 3% of the time, Pallas kernels for 0%

profile of v6, /device:TPU:1, one launch (start us, length us, event | category | flops | bytes accessed | tf_op | source)
XLA Modules:
  0.0 152.7 jit_solution(5214041282920367007)
XLA Ops:
  0.6 1.2 reshape.196
  1.9 0.5 slice_reduce_fusion.1
  2.5 0.9 broadcast_in_dim.49
  3.4 11.6 %all-to-all-start = ((bf16[64,32,128]{2,1,0:T(8,128)(2,1)}), bf16[64,32,128]{2,1,0:T(8,128)(2,1)S(1)}, u32[]{:S(2)}, u32[]{:S(2)}) async-start(bf16[64,32,128]{2,1,0:T(8,128)(2,1)} %broadcast_in_dim.49), calls=%async_computation | async-start | bytes 1048576 | tf_op jit(solution)/shard_map/all_to_all | solution.py:98
  15.6 16.7 %all-to-all-done = bf16[64,32,128]{2,1,0:T(8,128)(2,1)S(1)} async-done(((bf16[64,32,128]{2,1,0:T(8,128)(2,1)}), bf16[64,32,128]{2,1,0:T(8,128)(2,1)S(1)}, u32[]{:S(2)}, u32[]{:S(2)}) %all-to-all-start) | async-done | bytes 524320 | tf_op jit(solution)/shard_map/all_to_all | solution.py:98
  32.3 0.4 reshape_reshape_reshape_reshape.6
  32.7 0.6 gather_fusion
  33.6 0.2 copy.401
  33.8 0.2 copy.400
  34.0 0.8 fusion.34
  35.1 0.4 reshape.201
  35.7 27.9 %all_to_all.25 = bf16[8,259,128]{2,1,0:T(8,128)(2,1)S(1)} all-to-all(bf16[8,259,128]{2,1,0:T(8,128)(2,1)S(1)} %pad_maximum_fusion.2), channel_id=1, replica_groups=mesh['space'=64,'chan'=8] {'chan'}, dimensions={0} | all-to-all | bytes 1060864 | tf_op jit(solution)/shard_map/all_to_all | solution.py:98
  63.8 0.3 reshape_reshape.21
  64.5 0.2 reshape.209
  64.7 0.2 copy.421
  65.1 0.6 reshape.204
  65.8 0.4 copy.427
  66.2 0.4 copy.457
  66.6 0.4 pad.76.clone
  67.0 0.5 fusion.14
  67.5 0.3 convolution_select_fusion.1
  67.8 0.4 copy.425
  68.2 0.7 add_multiply_fusion
  68.9 0.2 copy.426
  69.1 1.7 %fusion.35 = f32[128,3,3,64]{3,0,2,1:T(8,128)S(1)} fusion(bf16[2,64,10,66]{1,0,3,2:T(2,128)(2,1)S(1)} %copy.427, bf16[8,2,64,128]{3,0,2,1:T(8,128)(2,1)S(1)} %fusion.7), kind=kOutput, calls=%fused_computation.76 | convolution fusion | flops 150994944 | bytes 726016 | tf_op jit(solution)/shard_map/transpose | solution.py:181
  70.9 0.2 reshape.210
  71.2 0.4 copy-done.7
  71.6 1.0 fusion
  72.7 0.2 reshape.249
  73.0 0.2 copy.436
  73.2 0.2 copy.437
  73.5 0.4 reshape.212
  74.0 0.2 broadcast_select_fusion
  74.5 0.2 convolution_convert_fusion
  74.8 0.2 copy.416
  75.0 0.2 reshape.207
  75.3 0.6 fusion.25
  75.9 0.2 copy.422
  76.1 0.2 reshape_reshape.25
  76.6 25.4 %all_to_all.26 = bf16[8,387,128]{2,1,0:T(8,128)(2,1)S(1)} all-to-all(bf16[8,387,128]{2,1,0:T(8,128)(2,1)S(1)} %pad_maximum_fusion), channel_id=1, replica_groups=mesh['space'=64,'chan'=8] {'chan'}, dimensions={0} | all-to-all | bytes 1585152 | tf_op jit(solution)/shard_map/all_to_all | solution.py:98
  102.1 0.5 reshape.256
  102.7 0.3 copy.442
  103.1 0.3 copy.444
  103.4 0.2 fusion.47
  103.9 0.4 copy.502
  104.3 0.2 fusion.4
  104.8 0.3 copy.456
  105.1 0.3 copy.446
  105.6 0.9 pad_maximum_fusion.1
  106.5 7.1 %all-to-all-start.3 = ((bf16[64,37,128]{2,1,0:T(8,128)(2,1)}), bf16[64,37,128]{2,1,0:T(8,128)(2,1)S(1)}, u32[]{:S(2)}, u32[]{:S(2)}) async-start(bf16[64,37,128]{2,1,0:T(8,128)(2,1)} %pad_maximum_fusion.1), calls=%async_computation.3 | async-start | bytes 1310720 | tf_op jit(solution)/shard_map/all_to_all | solution.py:98
  113.6 0.6 copy.510
  114.2 19.4 %all-to-all-done.3 = bf16[64,37,128]{2,1,0:T(8,128)(2,1)S(1)} async-done(((bf16[64,37,128]{2,1,0:T(8,128)(2,1)}), bf16[64,37,128]{2,1,0:T(8,128)(2,1)S(1)}, u32[]{:S(2)}, u32[]{:S(2)}) %all-to-all-start.3) | async-done | bytes 606240 | tf_op jit(solution)/shard_map/all_to_all | solution.py:98
  133.9 0.7 pad.75
  134.5 6.3 %all-to-all-start.4 = ((f32[64,3,128]{2,1,0:T(4,128)}), f32[64,3,128]{2,1,0:T(4,128)S(1)}, u32[]{:S(2)}, u32[]{:S(2)}) async-start(f32[64,3,128]{2,1,0:T(4,128)} %pad.75), calls=%async_computation.4 | async-start | bytes 262144 | tf_op jit(solution)/shard_map/all_to_all | solution.py:98
  140.9 0.4 reshape_reshape_reshape_reshape.7
  141.3 0.6 gather_fusion.1
  142.1 0.3 copy.448
  142.4 0.3 copy.449
  142.8 0.3 fusion.6
  143.1 0.3 copy.450
  143.4 0.9 reshape.221
  144.3 6.8 %all-to-all-done.4 = f32[64,3,128]{2,1,0:T(4,128)S(1)} async-done(((f32[64,3,128]{2,1,0:T(4,128)}), f32[64,3,128]{2,1,0:T(4,128)S(1)}, u32[]{:S(2)}, u32[]{:S(2)}) %all-to-all-start.4) | async-done | bytes 98336 | tf_op jit(solution)/shard_map/all_to_all | solution.py:98
  151.4 0.6 slice.250
  152.0 0.6 slice_bitcast_fusion.3
  (112 shorter events, 4.9 us)
Async XLA Ops:
  0.6 14.9 %copy-start = (bf16[2,16,1024]{2,1,0:T(8,128)(2,1)S(1)}, bf16[2,16,1024]{2,1,0:T(8,128)(2,1)}, u32[]{:S(2)}) copy-start(bf16[2,16,1024]{2,1,0:T(8,128)(2,1)} %param.11) | copy-start | bytes 196612
  1.9 13.2 %copy-start.5 = (s32[2,4]{1,0:T(2,128)S(1)}, s32[2,4]{1,0:T(2,128)}, u32[]{:S(2)}) copy-start(s32[2,4]{1,0:T(2,128)} %param.12) | copy-start | bytes 100
  1.9 13.2 %copy-start.2 = (bf16[16,4,128]{2,1,0:T(4,128)(2,1)S(1)}, bf16[16,4,128]{2,1,0:T(4,128)(2,1)}, u32[]{:S(2)}) copy-start(bf16[16,4,128]{2,1,0:T(4,128)(2,1)} %param.10) | copy-start | bytes 49156
  1.9 13.2 %copy-start.1 = (bf16[16,9,64]{2,0,1:T(8,128)(2,1)S(1)}, bf16[16,9,64]{2,0,1:T(8,128)(2,1)}, u32[]{:S(2)}) copy-start(bf16[16,9,64]{2,0,1:T(8,128)(2,1)} %param.9) | copy-start | bytes 55300
  2.4 13.1 %copy-start.6 = (s32[2,4]{1,0:T(2,128)S(1)}, s32[2,4]{1,0:T(2,128)}, u32[]{:S(2)}) copy-start(s32[2,4]{1,0:T(2,128)} %param.13) | copy-start | bytes 100
  3.4 28.9 %all-to-all-start = ((bf16[64,32,128]{2,1,0:T(8,128)(2,1)}), bf16[64,32,128]{2,1,0:T(8,128)(2,1)S(1)}, u32[]{:S(2)}, u32[]{:S(2)}) async-start(bf16[64,32,128]{2,1,0:T(8,128)(2,1)} %broadcast_in_dim.49), calls=%async_computation | async-start | bytes 1048576 | tf_op jit(solution)/shard_map/all_to_all | solution.py:98
  66.2 1.3 copy-start.4
  67.5 0.7 copy-start.3
  70.9 0.7 copy-start.7
  106.5 27.2 %all-to-all-start.3 = ((bf16[64,37,128]{2,1,0:T(8,128)(2,1)}), bf16[64,37,128]{2,1,0:T(8,128)(2,1)S(1)}, u32[]{:S(2)}, u32[]{:S(2)}) async-start(bf16[64,37,128]{2,1,0:T(8,128)(2,1)} %pad_maximum_fusion.1), calls=%async_computation.3 | async-start | bytes 1310720 | tf_op jit(solution)/shard_map/all_to_all | solution.py:98
  134.5 16.6 %all-to-all-start.4 = ((f32[64,3,128]{2,1,0:T(4,128)}), f32[64,3,128]{2,1,0:T(4,128)S(1)}, u32[]{:S(2)}, u32[]{:S(2)}) async-start(f32[64,3,128]{2,1,0:T(4,128)} %pad.75), calls=%async_computation.4 | async-start | bytes 262144 | tf_op jit(solution)/shard_map/all_to_all | solution.py:98

commit v7 on v6

--- a/solution.py
+++ b/solution.py
@@ -136,7 +136,10 @@
     )
 
     images = features.reshape(tiles, share, S, S)
-    strips = edge_strips(images)
+    flat_in = features
+    strips = jnp.stack(
+        [flat_in[..., :S], flat_in[..., S - 1 :: S], flat_in[..., S * (S - 1) :], flat_in[..., ::S]], axis=1
+    )
     (strips_all,) = exchange([to_all(strips, n_space)], "space")
     halo = bordering(strips_all.reshape((n_space * tiles,) + strips.shape[1:]), partner, orientation)
     padded = pad_cat(images, halo)

time: 153 us -> 155 us (1.013)
    slice x2, local copies, waits for them, and re-layouts: 0.49 us -> 2.21 us  [the longest x1 1.15 us: shards(): flat_in[..., S - 1::S]]
where the time goes in v7:
time: 155 us; the launch traced here: 154 us
  blocking collectives  53.3 us (34%)
  waiting for transfers between devices  42.8 us (28%)
  starting transfers between devices  24.9 us (16%)
  local copies, waits for them, and re-layouts  22.3 us (14%)
  other arithmetic  4.57 us (3%)
  matrix products  4.51 us (3%)
  between operations  1.62 us (1%)
    all_to_all x2, blocking collectives, exchange(): got = lax.all_to_all(jnp.concatenate(flat, axis=1), axis, 0, 0, tiled=True)  53.3 us
    all_to_all x3, waiting for transfers between devices, exchange(): got = lax.all_to_all(jnp.concatenate(flat, axis=1), axis, 0, 0, tiled=True)  42.8 us
    all_to_all x3, starting transfers between devices, exchange(): got = lax.all_to_all(jnp.concatenate(flat, axis=1), axis, 0, 0, tiled=True)  24.9 us
  transfers between devices with their start and end apart: 3, of which 3 were waited for; matrix products, arithmetic and copies ran while one was open for 3% of the time, Pallas kernels for 0%

profile of v7, /device:TPU:1, one launch (start us, length us, event | category | flops | bytes accessed | tf_op | source)
XLA Modules:
  0.0 154.0 jit_solution(15356609384459593270)
XLA Ops:
  0.7 1.2 slice.145
  1.8 1.1 slice.147
  2.9 0.8 slice_bitcast_fusion.15
  3.8 0.9 broadcast_in_dim.49
  4.7 11.6 %all-to-all-start = ((bf16[64,32,128]{2,1,0:T(8,128)(2,1)}), bf16[64,32,128]{2,1,0:T(8,128)(2,1)S(1)}, u32[]{:S(2)}, u32[]{:S(2)}) async-start(bf16[64,32,128]{2,1,0:T(8,128)(2,1)} %broadcast_in_dim.49), calls=%async_computation | async-start | bytes 1048576 | tf_op jit(solution)/shard_map/all_to_all | solution.py:98
  16.3 0.2 reshape.198
  17.1 16.5 %all-to-all-done = bf16[64,32,128]{2,1,0:T(8,128)(2,1)S(1)} async-done(((bf16[64,32,128]{2,1,0:T(8,128)(2,1)}), bf16[64,32,128]{2,1,0:T(8,128)(2,1)S(1)}, u32[]{:S(2)}, u32[]{:S(2)}) %all-to-all-start) | async-done | bytes 524320 | tf_op jit(solution)/shard_map/all_to_all | solution.py:98
  33.6 0.4 reshape_reshape_reshape_reshape.6
  34.0 0.6 gather_fusion
  34.9 0.2 copy.173
  35.2 0.2 copy.172
  35.4 0.8 fusion.29
  36.5 0.4 reshape.201
  37.1 27.9 %all_to_all.25 = bf16[8,259,128]{2,1,0:T(8,128)(2,1)S(1)} all-to-all(bf16[8,259,128]{2,1,0:T(8,128)(2,1)S(1)} %pad_maximum_fusion.2), channel_id=1, replica_groups=mesh['space'=64,'chan'=8] {'chan'}, dimensions={0} | all-to-all | bytes 1060864 | tf_op jit(solution)/shard_map/all_to_all | solution.py:98
  65.1 0.3 reshape_reshape.21
  66.4 0.6 reshape.204
  67.1 0.4 copy.199
  67.5 0.4 copy.226
  67.9 0.4 pad.76.clone
  68.4 0.5 fusion.12
  68.9 0.3 convolution_select_fusion.1
  69.1 0.4 copy.197
  69.5 0.7 add_multiply_fusion
  70.2 0.2 copy.198
  70.5 1.7 %fusion.30 = f32[128,3,3,64]{3,0,2,1:T(8,128)S(1)} fusion(bf16[2,64,10,66]{1,0,3,2:T(2,128)(2,1)S(1)} %copy.199, bf16[8,2,64,128]{3,0,2,1:T(8,128)(2,1)S(1)} %fusion.7), kind=kOutput, calls=%fused_computation.67 | convolution fusion | flops 150994944 | bytes 726016 | tf_op jit(solution)/shard_map/transpose | solution.py:184
  72.2 0.2 reshape.210
  72.5 0.4 copy-done.8
  72.9 1.0 fusion
  74.1 0.2 reshape.249
  74.3 0.2 copy.208
  74.6 0.2 copy.209
  74.8 0.4 reshape.212
  75.3 0.2 broadcast_select_fusion
  75.9 0.2 convolution_convert_fusion
  76.2 0.2 copy.188
  76.4 0.2 reshape.207
  76.6 0.6 fusion.23
  77.3 0.2 copy.194
  77.5 0.2 reshape_reshape.25
  78.0 25.4 %all_to_all.26 = bf16[8,387,128]{2,1,0:T(8,128)(2,1)S(1)} all-to-all(bf16[8,387,128]{2,1,0:T(8,128)(2,1)S(1)} %pad_maximum_fusion), channel_id=1, replica_groups=mesh['space'=64,'chan'=8] {'chan'}, dimensions={0} | all-to-all | bytes 1585152 | tf_op jit(solution)/shard_map/all_to_all | solution.py:98
  103.4 0.5 reshape.256
  104.1 0.3 copy.214
  104.5 0.3 copy.216
  104.8 0.2 fusion.42
  105.3 0.4 copy.267
  105.7 0.2 fusion.4
  106.2 0.3 copy.225
  106.5 0.3 copy.218
  107.0 0.9 pad_maximum_fusion.1
  107.9 7.1 %all-to-all-start.3 = ((bf16[64,37,128]{2,1,0:T(8,128)(2,1)}), bf16[64,37,128]{2,1,0:T(8,128)(2,1)S(1)}, u32[]{:S(2)}, u32[]{:S(2)}) async-start(bf16[64,37,128]{2,1,0:T(8,128)(2,1)} %pad_maximum_fusion.1), calls=%async_computation.3 | async-start | bytes 1310720 | tf_op jit(solution)/shard_map/all_to_all | solution.py:98
  115.0 0.6 copy.275
  115.6 19.4 %all-to-all-done.3 = bf16[64,37,128]{2,1,0:T(8,128)(2,1)S(1)} async-done(((bf16[64,37,128]{2,1,0:T(8,128)(2,1)}), bf16[64,37,128]{2,1,0:T(8,128)(2,1)S(1)}, u32[]{:S(2)}, u32[]{:S(2)}) %all-to-all-start.3) | async-done | bytes 606240 | tf_op jit(solution)/shard_map/all_to_all | solution.py:98
  135.2 0.7 pad.75
  135.9 6.3 %all-to-all-start.4 = ((f32[64,3,128]{2,1,0:T(4,128)}), f32[64,3,128]{2,1,0:T(4,128)S(1)}, u32[]{:S(2)}, u32[]{:S(2)}) async-start(f32[64,3,128]{2,1,0:T(4,128)} %pad.75), calls=%async_computation.4 | async-start | bytes 262144 | tf_op jit(solution)/shard_map/all_to_all | solution.py:98
  142.2 0.4 reshape_reshape_reshape_reshape.7
  142.6 0.6 gather_fusion.1
  143.5 0.3 copy.220
  143.8 0.3 copy.221
  144.1 0.3 fusion.6
  144.5 0.3 copy.222
  144.7 0.9 reshape.221
  145.7 6.8 %all-to-all-done.4 = f32[64,3,128]{2,1,0:T(4,128)S(1)} async-done(((f32[64,3,128]{2,1,0:T(4,128)}), f32[64,3,128]{2,1,0:T(4,128)S(1)}, u32[]{:S(2)}, u32[]{:S(2)}) %all-to-all-start.4) | async-done | bytes 98336 | tf_op jit(solution)/shard_map/all_to_all | solution.py:98
  152.8 0.6 slice.246
  153.4 0.6 slice_bitcast_fusion.3
  (116 shorter events, 5.3 us)
Async XLA Ops:
  0.6 16.4 %copy-start = (bf16[2,16,1024]{2,1,0:T(8,128)(2,1)S(1)}, bf16[2,16,1024]{2,1,0:T(8,128)(2,1)}, u32[]{:S(2)}) copy-start(bf16[2,16,1024]{2,1,0:T(8,128)(2,1)} %param.11) | copy-start | bytes 196612
  0.6 15.6 %copy-start.1 = (bf16[2,8,4096]{2,1,0:T(8,128)(2,1)S(1)}, bf16[2,8,4096]{2,1,0:T(8,128)(2,1)}, u32[]{:S(2)}) copy-start(bf16[2,8,4096]{2,1,0:T(8,128)(2,1)} %param.8) | copy-start | bytes 393220
  0.7 15.9 %copy-start.6 = (s32[2,4]{1,0:T(2,128)S(1)}, s32[2,4]{1,0:T(2,128)}, u32[]{:S(2)}) copy-start(s32[2,4]{1,0:T(2,128)} %param.12) | copy-start | bytes 100
  0.7 16.0 %copy-start.3 = (bf16[16,4,128]{2,1,0:T(4,128)(2,1)S(1)}, bf16[16,4,128]{2,1,0:T(4,128)(2,1)}, u32[]{:S(2)}) copy-start(bf16[16,4,128]{2,1,0:T(4,128)(2,1)} %param.10) | copy-start | bytes 49156
  0.7 16.0 %copy-start.2 = (bf16[16,9,64]{2,0,1:T(8,128)(2,1)S(1)}, bf16[16,9,64]{2,0,1:T(8,128)(2,1)}, u32[]{:S(2)}) copy-start(bf16[16,9,64]{2,0,1:T(8,128)(2,1)} %param.9) | copy-start | bytes 55300
  3.8 13.2 %copy-start.7 = (s32[2,4]{1,0:T(2,128)S(1)}, s32[2,4]{1,0:T(2,128)}, u32[]{:S(2)}) copy-start(s32[2,4]{1,0:T(2,128)} %param.13) | copy-start | bytes 100
  4.7 28.9 %all-to-all-start = ((bf16[64,32,128]{2,1,0:T(8,128)(2,1)}), bf16[64,32,128]{2,1,0:T(8,128)(2,1)S(1)}, u32[]{:S(2)}, u32[]{:S(2)}) async-start(bf16[64,32,128]{2,1,0:T(8,128)(2,1)} %broadcast_in_dim.49), calls=%async_computation | async-start | bytes 1048576 | tf_op jit(solution)/shard_map/all_to_all | solution.py:98
  67.5 1.3 copy-start.5
  68.8 0.7 copy-start.4
  72.2 0.7 copy-start.8
  107.9 27.2 %all-to-all-start.3 = ((bf16[64,37,128]{2,1,0:T(8,128)(2,1)}), bf16[64,37,128]{2,1,0:T(8,128)(2,1)S(1)}, u32[]{:S(2)}, u32[]{:S(2)}) async-start(bf16[64,37,128]{2,1,0:T(8,128)(2,1)} %pad_maximum_fusion.1), calls=%async_computation.3 | async-start | bytes 1310720 | tf_op jit(solution)/shard_map/all_to_all | solution.py:98
  135.9 16.6 %all-to-all-start.4 = ((f32[64,3,128]{2,1,0:T(4,128)}), f32[64,3,128]{2,1,0:T(4,128)S(1)}, u32[]{:S(2)}, u32[]{:S(2)}) async-start(f32[64,3,128]{2,1,0:T(4,128)} %pad.75), calls=%async_computation.4 | async-start | bytes 262144 | tf_op jit(solution)/shard_map/all_to_all | solution.py:98

commit v8 on v6

--- a/solution.py
+++ b/solution.py
@@ -207,7 +207,7 @@
 
     rims = rim_strips(grad_padded)
     w_len = w_sum.shape[0]
-    piece = -(-w_len // n_space)
+    piece = -(-w_len // (n_space * 128)) * 128
     w_pieces = jnp.pad(w_sum, (0, piece * n_space - w_len)).reshape(n_space, piece)
     rims_all, w_got = exchange([to_all(rims.astype(BF16), n_space), split_wide(w_pieces)], "space")
     grad_scale = float(n_space * tiles * S * S) ** (-0.5)

time: 153 us -> 153 us (level)
  no operation moved by 1% of the time
where the time goes in v8:
time: 153 us; the launch traced here: 152 us
  blocking collectives  53.3 us (35%)
  waiting for transfers between devices  43 us (28%)
  starting transfers between devices  25 us (16%)
  local copies, waits for them, and re-layouts  20.6 us (13%)
  matrix products  4.5 us (3%)
  other arithmetic  4.45 us (3%)
  between operations  1.59 us (1%)
    all_to_all x2, blocking collectives, exchange(): got = lax.all_to_all(jnp.concatenate(flat, axis=1), axis, 0, 0, tiled=True)  53.3 us
    all_to_all x3, waiting for transfers between devices, exchange(): got = lax.all_to_all(jnp.concatenate(flat, axis=1), axis, 0, 0, tiled=True)  43 us
    all_to_all x3, starting transfers between devices, exchange(): got = lax.all_to_all(jnp.concatenate(flat, axis=1), axis, 0, 0, tiled=True)  25 us
  transfers between devices with their start and end apart: 3, of which 3 were waited for; matrix products, arithmetic and copies ran while one was open for 3% of the time, Pallas kernels for 0%

profile of v8, /device:TPU:1, one launch (start us, length us, event | category | flops | bytes accessed | tf_op | source)
XLA Modules:
  0.0 152.4 jit_solution(9970523479884931482)
XLA Ops:
  0.6 1.2 reshape.198
  1.9 0.5 slice_reduce_fusion.1
  2.5 0.9 broadcast_in_dim.51
  3.4 11.6 %all-to-all-start = ((bf16[64,32,128]{2,1,0:T(8,128)(2,1)}), bf16[64,32,128]{2,1,0:T(8,128)(2,1)S(1)}, u32[]{:S(2)}, u32[]{:S(2)}) async-start(bf16[64,32,128]{2,1,0:T(8,128)(2,1)} %broadcast_in_dim.51), calls=%async_computation | async-start | bytes 1048576 | tf_op jit(solution)/shard_map/all_to_all | solution.py:98
  15.6 16.7 %all-to-all-done = bf16[64,32,128]{2,1,0:T(8,128)(2,1)S(1)} async-done(((bf16[64,32,128]{2,1,0:T(8,128)(2,1)}), bf16[64,32,128]{2,1,0:T(8,128)(2,1)S(1)}, u32[]{:S(2)}, u32[]{:S(2)}) %all-to-all-start) | async-done | bytes 524320 | tf_op jit(solution)/shard_map/all_to_all | solution.py:98
  32.3 0.4 reshape_reshape_reshape_reshape.6
  32.7 0.6 gather_fusion
  33.6 0.2 copy.401
  33.8 0.2 copy.400
  34.1 0.8 fusion.34
  35.1 0.4 reshape.203
  35.7 27.9 %all_to_all.25 = bf16[8,259,128]{2,1,0:T(8,128)(2,1)S(1)} all-to-all(bf16[8,259,128]{2,1,0:T(8,128)(2,1)S(1)} %pad_maximum_fusion.2), channel_id=1, replica_groups=mesh['space'=64,'chan'=8] {'chan'}, dimensions={0} | all-to-all | bytes 1060864 | tf_op jit(solution)/shard_map/all_to_all | solution.py:98
  63.8 0.3 reshape_reshape.22
  64.5 0.2 reshape.211
  64.7 0.2 copy.421
  65.1 0.6 reshape.206
  65.8 0.4 copy.427
  66.2 0.4 copy.457
  66.6 0.4 pad.65.clone
  67.0 0.5 fusion.14
  67.5 0.3 convolution_select_fusion.1
  67.8 0.4 copy.425
  68.2 0.7 add_multiply_fusion
  68.9 0.2 copy.426
  69.1 1.7 %fusion.35 = f32[128,3,3,64]{3,0,2,1:T(8,128)S(1)} fusion(bf16[2,64,10,66]{1,0,3,2:T(2,128)(2,1)S(1)} %copy.427, bf16[8,2,64,128]{3,0,2,1:T(8,128)(2,1)S(1)} %fusion.7), kind=kOutput, calls=%fused_computation.76 | convolution fusion | flops 150994944 | bytes 726016 | tf_op jit(solution)/shard_map/transpose | solution.py:181
  70.9 0.2 reshape.212
  71.2 0.4 copy-done.7
  71.6 1.0 fusion
  72.7 0.2 reshape.248
  73.0 0.2 copy.436
  73.2 0.2 copy.437
  73.5 0.4 reshape.214
  74.0 0.2 broadcast_select_fusion
  74.5 0.2 convolution_convert_fusion
  74.8 0.2 copy.416
  75.0 0.2 reshape.209
  75.3 0.6 fusion.25
  75.9 0.2 copy.422
  76.1 0.2 reshape_reshape.26
  76.6 25.4 %all_to_all.26 = bf16[8,387,128]{2,1,0:T(8,128)(2,1)S(1)} all-to-all(bf16[8,387,128]{2,1,0:T(8,128)(2,1)S(1)} %pad_maximum_fusion), channel_id=1, replica_groups=mesh['space'=64,'chan'=8] {'chan'}, dimensions={0} | all-to-all | bytes 1585152 | tf_op jit(solution)/shard_map/all_to_all | solution.py:98
  102.1 0.5 reshape.255
  102.7 0.3 copy.442
  103.1 0.3 copy.444
  103.4 0.2 fusion.44
  103.9 0.4 copy.500
  104.3 0.2 fusion.4
  104.6 0.3 copy.456
  104.9 0.3 copy.446
  105.4 1.0 pad_maximum_fusion.1
  106.3 7.1 %all-to-all-start.3 = ((bf16[64,38,128]{2,1,0:T(8,128)(2,1)}), bf16[64,38,128]{2,1,0:T(8,128)(2,1)S(1)}, u32[]{:S(2)}, u32[]{:S(2)}) async-start(bf16[64,38,128]{2,1,0:T(8,128)(2,1)} %pad_maximum_fusion.1), calls=%async_computation.3 | async-start | bytes 1310720 | tf_op jit(solution)/shard_map/all_to_all | solution.py:98
  113.4 0.6 copy.507
  114.1 19.4 %all-to-all-done.3 = bf16[64,38,128]{2,1,0:T(8,128)(2,1)S(1)} async-done(((bf16[64,38,128]{2,1,0:T(8,128)(2,1)}), bf16[64,38,128]{2,1,0:T(8,128)(2,1)S(1)}, u32[]{:S(2)}, u32[]{:S(2)}) %all-to-all-start.3) | async-done | bytes 622624 | tf_op jit(solution)/shard_map/all_to_all | solution.py:98
  133.6 0.7 broadcast_in_dim.53
  134.3 6.3 %all-to-all-start.4 = ((f32[64,3,128]{2,1,0:T(4,128)}), f32[64,3,128]{2,1,0:T(4,128)S(1)}, u32[]{:S(2)}, u32[]{:S(2)}) async-start(f32[64,3,128]{2,1,0:T(4,128)} %broadcast_in_dim.53), calls=%async_computation.4 | async-start | bytes 262144 | tf_op jit(solution)/shard_map/all_to_all | solution.py:98
  140.6 0.4 reshape_reshape_reshape_reshape.7
  141.0 0.6 gather_fusion.1
  141.9 0.3 copy.448
  142.2 0.3 copy.449
  142.5 0.3 fusion.6
  142.9 0.3 copy.450
  143.1 0.9 reshape.222
  144.1 6.8 %all-to-all-done.4 = f32[64,3,128]{2,1,0:T(4,128)S(1)} async-done(((f32[64,3,128]{2,1,0:T(4,128)}), f32[64,3,128]{2,1,0:T(4,128)S(1)}, u32[]{:S(2)}, u32[]{:S(2)}) %all-to-all-start.4) | async-done | bytes 98336 | tf_op jit(solution)/shard_map/all_to_all | solution.py:98
  151.0 0.6 slice.243
  151.7 0.6 slice_bitcast_fusion.3
  (108 shorter events, 4.5 us)
Async XLA Ops:
  0.6 14.9 %copy-start = (bf16[2,16,1024]{2,1,0:T(8,128)(2,1)S(1)}, bf16[2,16,1024]{2,1,0:T(8,128)(2,1)}, u32[]{:S(2)}) copy-start(bf16[2,16,1024]{2,1,0:T(8,128)(2,1)} %param.11) | copy-start | bytes 196612
  1.9 13.2 %copy-start.5 = (s32[2,4]{1,0:T(2,128)S(1)}, s32[2,4]{1,0:T(2,128)}, u32[]{:S(2)}) copy-start(s32[2,4]{1,0:T(2,128)} %param.12) | copy-start | bytes 100
  1.9 13.2 %copy-start.2 = (bf16[16,4,128]{2,1,0:T(4,128)(2,1)S(1)}, bf16[16,4,128]{2,1,0:T(4,128)(2,1)}, u32[]{:S(2)}) copy-start(bf16[16,4,128]{2,1,0:T(4,128)(2,1)} %param.10) | copy-start | bytes 49156
  1.9 13.2 %copy-start.1 = (bf16[16,9,64]{2,0,1:T(8,128)(2,1)S(1)}, bf16[16,9,64]{2,0,1:T(8,128)(2,1)}, u32[]{:S(2)}) copy-start(bf16[16,9,64]{2,0,1:T(8,128)(2,1)} %param.9) | copy-start | bytes 55300
  2.4 13.1 %copy-start.6 = (s32[2,4]{1,0:T(2,128)S(1)}, s32[2,4]{1,0:T(2,128)}, u32[]{:S(2)}) copy-start(s32[2,4]{1,0:T(2,128)} %param.13) | copy-start | bytes 100
  3.4 28.9 %all-to-all-start = ((bf16[64,32,128]{2,1,0:T(8,128)(2,1)}), bf16[64,32,128]{2,1,0:T(8,128)(2,1)S(1)}, u32[]{:S(2)}, u32[]{:S(2)}) async-start(bf16[64,32,128]{2,1,0:T(8,128)(2,1)} %broadcast_in_dim.51), calls=%async_computation | async-start | bytes 1048576 | tf_op jit(solution)/shard_map/all_to_all | solution.py:98
  66.2 1.3 copy-start.4
  67.5 0.7 copy-start.3
  70.9 0.7 copy-start.7
  106.3 27.2 %all-to-all-start.3 = ((bf16[64,38,128]{2,1,0:T(8,128)(2,1)}), bf16[64,38,128]{2,1,0:T(8,128)(2,1)S(1)}, u32[]{:S(2)}, u32[]{:S(2)}) async-start(bf16[64,38,128]{2,1,0:T(8,128)(2,1)} %pad_maximum_fusion.1), calls=%async_computation.3 | async-start | bytes 1310720 | tf_op jit(solution)/shard_map/all_to_all | solution.py:98
  134.3 16.6 %all-to-all-start.4 = ((f32[64,3,128]{2,1,0:T(4,128)}), f32[64,3,128]{2,1,0:T(4,128)S(1)}, u32[]{:S(2)}, u32[]{:S(2)}) async-start(f32[64,3,128]{2,1,0:T(4,128)} %broadcast_in_dim.53), calls=%async_computation.4 | async-start | bytes 262144 | tf_op jit(solution)/shard_map/all_to_all | solution.py:98

commit v9 on v8

--- a/solution.py
+++ b/solution.py
@@ -179,11 +179,10 @@
         block, grad_pre, (1, 1), "VALID", dimension_numbers=swapped, preferred_element_type=F32
     )
     conv_part = conv_part.transpose(1, 2, 3, 0).reshape(out_channels, conv_cols)
-    w_back_conv = jnp.flip(w_conv, (2, 3)).transpose(1, 0, 2, 3)
-    grad_block = lax.conv_general_dilated(
-        grad_pre, w_back_conv, (1, 1), ((2, 2), (2, 2)), dimension_numbers=plain,
-        preferred_element_type=F32,
-    )
+    _, data_grad = jax.vjp(
+        lambda x: lax.conv_general_dilated(x, w_conv, (1, 1), "VALID", dimension_numbers=plain), block
+    )
+    (grad_block,) = data_grad(grad_pre)
 
     pooled_out = jnp.moveaxis(pooled_rows.reshape(tiles, n_chan, out_share, rows // 2 * half), 1, 0)
     grad_out = jnp.moveaxis(

time: 153 us -> 153 us (level)
  no operation moved by 1% of the time
where the time goes in v9:
time: 153 us; the launch traced here: 152 us
  blocking collectives  53.3 us (35%)
  waiting for transfers between devices  43 us (28%)
  starting transfers between devices  25 us (16%)
  local copies, waits for them, and re-layouts  20.6 us (13%)
  matrix products  4.5 us (3%)
  other arithmetic  4.45 us (3%)
  between operations  1.59 us (1%)
    all_to_all x2, blocking collectives, exchange(): got = lax.all_to_all(jnp.concatenate(flat, axis=1), axis, 0, 0, tiled=True)  53.3 us
    all_to_all x3, waiting for transfers between devices, exchange(): got = lax.all_to_all(jnp.concatenate(flat, axis=1), axis, 0, 0, tiled=True)  43 us
    all_to_all x3, starting transfers between devices, exchange(): got = lax.all_to_all(jnp.concatenate(flat, axis=1), axis, 0, 0, tiled=True)  25 us
  transfers between devices with their start and end apart: 3, of which 3 were waited for; matrix products, arithmetic and copies ran while one was open for 3% of the time, Pallas kernels for 0%

profile of v9, /device:TPU:1, one launch (start us, length us, event | category | flops | bytes accessed | tf_op | source)
XLA Modules:
  0.0 152.4 jit_solution(12994125994454679473)
XLA Ops:
  0.6 1.2 reshape.198
  1.9 0.5 slice_reduce_fusion.1
  2.5 0.9 broadcast_in_dim.51
  3.4 11.6 %all-to-all-start = ((bf16[64,32,128]{2,1,0:T(8,128)(2,1)}), bf16[64,32,128]{2,1,0:T(8,128)(2,1)S(1)}, u32[]{:S(2)}, u32[]{:S(2)}) async-start(bf16[64,32,128]{2,1,0:T(8,128)(2,1)} %broadcast_in_dim.51), calls=%async_computation | async-start | bytes 1048576 | tf_op jit(solution)/shard_map/all_to_all | solution.py:98
  15.6 16.7 %all-to-all-done = bf16[64,32,128]{2,1,0:T(8,128)(2,1)S(1)} async-done(((bf16[64,32,128]{2,1,0:T(8,128)(2,1)}), bf16[64,32,128]{2,1,0:T(8,128)(2,1)S(1)}, u32[]{:S(2)}, u32[]{:S(2)}) %all-to-all-start) | async-done | bytes 524320 | tf_op jit(solution)/shard_map/all_to_all | solution.py:98
  32.3 0.4 reshape_reshape_reshape_reshape.6
  32.7 0.6 gather_fusion
  33.6 0.2 copy.401
  33.8 0.2 copy.400
  34.1 0.8 fusion.33
  35.1 0.4 reshape.203
  35.7 27.9 %all_to_all.25 = bf16[8,259,128]{2,1,0:T(8,128)(2,1)S(1)} all-to-all(bf16[8,259,128]{2,1,0:T(8,128)(2,1)S(1)} %pad_maximum_fusion.2), channel_id=1, replica_groups=mesh['space'=64,'chan'=8] {'chan'}, dimensions={0} | all-to-all | bytes 1060864 | tf_op jit(solution)/shard_map/all_to_all | solution.py:98
  63.8 0.3 reshape_reshape.22
  64.5 0.2 reshape.211
  64.7 0.2 copy.421
  65.1 0.6 reshape.206
  65.8 0.4 copy.427
  66.2 0.4 copy.457
  66.6 0.4 pad.65.clone
  67.0 0.5 fusion.13
  67.5 0.3 convolution_select_fusion
  67.8 0.4 copy.425
  68.2 0.7 add_multiply_fusion
  68.9 0.2 copy.426
  69.1 1.7 %fusion.34 = f32[128,3,3,64]{3,0,2,1:T(8,128)S(1)} fusion(bf16[2,64,10,66]{1,0,3,2:T(2,128)(2,1)S(1)} %copy.427, bf16[8,2,64,128]{3,0,2,1:T(8,128)(2,1)S(1)} %fusion.6), kind=kOutput, calls=%fused_computation.75 | convolution fusion | flops 150994944 | bytes 726016 | tf_op jit(solution)/shard_map/transpose | solution.py:181
  70.9 0.2 reshape.212
  71.2 0.4 copy-done.7
  71.6 1.0 convolution_select_fusion.2
  72.7 0.2 reshape.248
  73.0 0.2 copy.436
  73.2 0.2 copy.437
  73.5 0.4 reshape.214
  74.0 0.2 broadcast_select_fusion
  74.5 0.2 convolution_convert_fusion
  74.8 0.2 copy.416
  75.0 0.2 reshape.209
  75.3 0.6 fusion.24
  75.9 0.2 copy.422
  76.1 0.2 reshape_reshape.26
  76.6 25.4 %all_to_all.26 = bf16[8,387,128]{2,1,0:T(8,128)(2,1)S(1)} all-to-all(bf16[8,387,128]{2,1,0:T(8,128)(2,1)S(1)} %pad_maximum_fusion), channel_id=1, replica_groups=mesh['space'=64,'chan'=8] {'chan'}, dimensions={0} | all-to-all | bytes 1585152 | tf_op jit(solution)/shard_map/all_to_all | solution.py:98
  102.1 0.5 reshape.255
  102.7 0.3 copy.442
  103.1 0.3 copy.444
  103.4 0.2 fusion.43
  104.0 0.4 copy.500
  104.3 0.2 fusion.3
  104.6 0.3 copy.456
  104.9 0.3 copy.446
  105.4 1.0 pad_maximum_fusion.1
  106.3 7.1 %all-to-all-start.3 = ((bf16[64,38,128]{2,1,0:T(8,128)(2,1)}), bf16[64,38,128]{2,1,0:T(8,128)(2,1)S(1)}, u32[]{:S(2)}, u32[]{:S(2)}) async-start(bf16[64,38,128]{2,1,0:T(8,128)(2,1)} %pad_maximum_fusion.1), calls=%async_computation.3 | async-start | bytes 1310720 | tf_op jit(solution)/shard_map/all_to_all | solution.py:98
  113.4 0.6 copy.507
  114.1 19.4 %all-to-all-done.3 = bf16[64,38,128]{2,1,0:T(8,128)(2,1)S(1)} async-done(((bf16[64,38,128]{2,1,0:T(8,128)(2,1)}), bf16[64,38,128]{2,1,0:T(8,128)(2,1)S(1)}, u32[]{:S(2)}, u32[]{:S(2)}) %all-to-all-start.3) | async-done | bytes 622624 | tf_op jit(solution)/shard_map/all_to_all | solution.py:98
  133.6 0.7 broadcast_in_dim.53
  134.3 6.3 %all-to-all-start.4 = ((f32[64,3,128]{2,1,0:T(4,128)}), f32[64,3,128]{2,1,0:T(4,128)S(1)}, u32[]{:S(2)}, u32[]{:S(2)}) async-start(f32[64,3,128]{2,1,0:T(4,128)} %broadcast_in_dim.53), calls=%async_computation.4 | async-start | bytes 262144 | tf_op jit(solution)/shard_map/all_to_all | solution.py:98
  140.6 0.4 reshape_reshape_reshape_reshape.7
  141.0 0.6 gather_fusion.1
  141.9 0.3 copy.448
  142.2 0.3 copy.449
  142.5 0.3 fusion.5
  142.9 0.3 copy.450
  143.2 0.9 reshape.222
  144.1 6.8 %all-to-all-done.4 = f32[64,3,128]{2,1,0:T(4,128)S(1)} async-done(((f32[64,3,128]{2,1,0:T(4,128)}), f32[64,3,128]{2,1,0:T(4,128)S(1)}, u32[]{:S(2)}, u32[]{:S(2)}) %all-to-all-start.4) | async-done | bytes 98336 | tf_op jit(solution)/shard_map/all_to_all | solution.py:98
  151.0 0.6 slice.243
  151.8 0.6 slice_bitcast_fusion.3
  (108 shorter events, 4.5 us)
Async XLA Ops:
  0.6 14.9 %copy-start = (bf16[2,16,1024]{2,1,0:T(8,128)(2,1)S(1)}, bf16[2,16,1024]{2,1,0:T(8,128)(2,1)}, u32[]{:S(2)}) copy-start(bf16[2,16,1024]{2,1,0:T(8,128)(2,1)} %param.11) | copy-start | bytes 196612
  1.9 13.2 %copy-start.5 = (s32[2,4]{1,0:T(2,128)S(1)}, s32[2,4]{1,0:T(2,128)}, u32[]{:S(2)}) copy-start(s32[2,4]{1,0:T(2,128)} %param.12) | copy-start | bytes 100
  1.9 13.2 %copy-start.2 = (bf16[16,4,128]{2,1,0:T(4,128)(2,1)S(1)}, bf16[16,4,128]{2,1,0:T(4,128)(2,1)}, u32[]{:S(2)}) copy-start(bf16[16,4,128]{2,1,0:T(4,128)(2,1)} %param.10) | copy-start | bytes 49156
  1.9 13.2 %copy-start.1 = (bf16[16,9,64]{2,0,1:T(8,128)(2,1)S(1)}, bf16[16,9,64]{2,0,1:T(8,128)(2,1)}, u32[]{:S(2)}) copy-start(bf16[16,9,64]{2,0,1:T(8,128)(2,1)} %param.9) | copy-start | bytes 55300
  2.4 13.1 %copy-start.6 = (s32[2,4]{1,0:T(2,128)S(1)}, s32[2,4]{1,0:T(2,128)}, u32[]{:S(2)}) copy-start(s32[2,4]{1,0:T(2,128)} %param.13) | copy-start | bytes 100
  3.4 28.9 %all-to-all-start = ((bf16[64,32,128]{2,1,0:T(8,128)(2,1)}), bf16[64,32,128]{2,1,0:T(8,128)(2,1)S(1)}, u32[]{:S(2)}, u32[]{:S(2)}) async-start(bf16[64,32,128]{2,1,0:T(8,128)(2,1)} %broadcast_in_dim.51), calls=%async_computation | async-start | bytes 1048576 | tf_op jit(solution)/shard_map/all_to_all | solution.py:98
  66.2 1.3 copy-start.4
  67.5 0.7 copy-start.3
  70.9 0.7 copy-start.7
  106.3 27.2 %all-to-all-start.3 = ((bf16[64,38,128]{2,1,0:T(8,128)(2,1)}), bf16[64,38,128]{2,1,0:T(8,128)(2,1)S(1)}, u32[]{:S(2)}, u32[]{:S(2)}) async-start(bf16[64,38,128]{2,1,0:T(8,128)(2,1)} %pad_maximum_fusion.1), calls=%async_computation.3 | async-start | bytes 1310720 | tf_op jit(solution)/shard_map/all_to_all | solution.py:98
  134.3 16.6 %all-to-all-start.4 = ((f32[64,3,128]{2,1,0:T(4,128)}), f32[64,3,128]{2,1,0:T(4,128)S(1)}, u32[]{:S(2)}, u32[]{:S(2)}) async-start(f32[64,3,128]{2,1,0:T(4,128)} %broadcast_in_dim.53), calls=%async_computation.4 | async-start | bytes 262144 | tf_op jit(solution)/shard_map/all_to_all | solution.py:98

commit v10 on v8

--- a/solution.py
+++ b/solution.py
@@ -198,12 +198,11 @@
     w_sum = jnp.sum(join_wide(w_back), axis=0)
 
     g = grad_in.astype(F32)
-    main = jnp.moveaxis(g[:, :, :, :rows, :], 0, 2).reshape(tiles, share, S, S + 2)
-    extra = jnp.pad(g[:, :, :, rows:, :], ((0, 0), (0, 0), (0, 0), (0, rows - 2), (0, 0)))
-    extra = jnp.moveaxis(extra, 0, 2).reshape(tiles, share, S, S + 2)
-    grad_padded = jnp.pad(main, ((0, 0), (0, 0), (0, 2), (0, 0))) + jnp.pad(
-        extra, ((0, 0), (0, 0), (rows, 0), (0, 0))
-    )[:, :, : S + 2, :]
+    lead = jnp.concatenate([g[:1, :, :, :2, :], g[1:, :, :, :2, :] + g[:-1, :, :, rows:, :]], axis=0)
+    body = jnp.concatenate([lead, g[:, :, :, 2:rows, :]], axis=3)
+    grad_padded = jnp.concatenate(
+        [jnp.moveaxis(body, 0, 2).reshape(tiles, share, S, S + 2), g[-1, :, :, rows:, :]], axis=2
+    )
 
     rims = rim_strips(grad_padded)
     w_len = w_sum.shape[0]

time: 153 us -> 152 us (level)
  no operation moved by 1% of the time
where the time goes in v10:
time: 152 us
  blocking collectives  53.3 us (35%)
  waiting for transfers between devices  42.9 us (28%)
  starting transfers between devices  24.9 us (16%)
  local copies, waits for them, and re-layouts  20.1 us (13%)
  other arithmetic  4.7 us (3%)
  matrix products  4.46 us (3%)
  between operations  1.62 us (1%)
    all_to_all x2, blocking collectives, exchange(): got = lax.all_to_all(jnp.concatenate(flat, axis=1), axis, 0, 0, tiled=True)  53.3 us
    all_to_all x3, waiting for transfers between devices, exchange(): got = lax.all_to_all(jnp.concatenate(flat, axis=1), axis, 0, 0, tiled=True)  42.9 us
    all_to_all x3, starting transfers between devices, exchange(): got = lax.all_to_all(jnp.concatenate(flat, axis=1), axis, 0, 0, tiled=True)  24.9 us
  transfers between devices with their start and end apart: 3, of which 3 were waited for; matrix products, arithmetic and copies ran while one was open for 3% of the time, Pallas kernels for 0%

profile of v10, /device:TPU:1, one launch (start us, length us, event | category | flops | bytes accessed | tf_op | source)
XLA Modules:
  0.0 152.0 jit_solution(14058511635169537506)
XLA Ops:
  0.6 1.2 reshape.195
  1.9 0.5 slice_reduce_fusion.1
  2.5 0.9 broadcast_in_dim.51
  3.4 11.6 %all-to-all-start = ((bf16[64,32,128]{2,1,0:T(8,128)(2,1)}), bf16[64,32,128]{2,1,0:T(8,128)(2,1)S(1)}, u32[]{:S(2)}, u32[]{:S(2)}) async-start(bf16[64,32,128]{2,1,0:T(8,128)(2,1)} %broadcast_in_dim.51), calls=%async_computation | async-start | bytes 1048576 | tf_op jit(solution)/shard_map/all_to_all | solution.py:98
  15.6 16.7 %all-to-all-done = bf16[64,32,128]{2,1,0:T(8,128)(2,1)S(1)} async-done(((bf16[64,32,128]{2,1,0:T(8,128)(2,1)}), bf16[64,32,128]{2,1,0:T(8,128)(2,1)S(1)}, u32[]{:S(2)}, u32[]{:S(2)}) %all-to-all-start) | async-done | bytes 524320 | tf_op jit(solution)/shard_map/all_to_all | solution.py:98
  32.3 0.4 reshape_reshape_reshape_reshape.6
  32.7 0.6 gather_fusion
  33.6 0.2 copy.388
  33.8 0.2 copy.387
  34.1 0.8 fusion.34
  34.9 0.2 copy_bitcast_fusion.1
  35.1 0.4 reshape.200
  35.7 27.9 %all_to_all.25 = bf16[8,259,128]{2,1,0:T(8,128)(2,1)S(1)} all-to-all(bf16[8,259,128]{2,1,0:T(8,128)(2,1)S(1)} %pad_maximum_fusion.2), channel_id=1, replica_groups=mesh['space'=64,'chan'=8] {'chan'}, dimensions={0} | all-to-all | bytes 1060864 | tf_op jit(solution)/shard_map/all_to_all | solution.py:98
  63.8 0.3 reshape_reshape.22
  64.5 0.2 reshape.208
  64.7 0.2 copy.408
  64.9 0.2 copy.443
  65.1 0.6 reshape.203
  65.7 0.4 copy.414
  66.2 0.4 copy.442
  66.6 0.4 pad.50.clone
  67.0 0.5 fusion.14
  67.5 0.3 convolution_select_fusion.1
  67.8 0.4 copy.412
  68.2 0.7 add_multiply_fusion
  68.9 0.2 copy.413
  69.1 1.6 %fusion.35 = f32[128,3,3,64]{3,0,2,1:T(8,128)S(1)} fusion(bf16[2,64,10,66]{1,0,3,2:T(2,128)(2,1)S(1)} %copy.414, bf16[8,2,64,128]{3,0,2,1:T(8,128)(2,1)S(1)} %fusion.7), kind=kOutput, calls=%fused_computation.73 | convolution fusion | flops 150994944 | bytes 726016 | tf_op jit(solution)/shard_map/transpose | solution.py:181
  70.8 0.2 reshape.209
  71.1 0.4 copy-done.7
  71.5 1.0 fusion
  72.5 0.1 copy.422
  72.7 0.2 reshape.244
  72.9 0.2 copy.423
  73.2 0.2 copy.424
  73.4 0.4 reshape.211
  73.9 0.2 broadcast_select_fusion
  74.5 0.2 convolution_convert_fusion
  74.8 0.2 copy.403
  75.0 0.2 reshape.206
  75.2 0.6 fusion.25
  75.9 0.2 copy.409
  76.1 0.2 reshape_reshape.26
  76.6 25.4 %all_to_all.26 = bf16[8,387,128]{2,1,0:T(8,128)(2,1)S(1)} all-to-all(bf16[8,387,128]{2,1,0:T(8,128)(2,1)S(1)} %pad_maximum_fusion), channel_id=1, replica_groups=mesh['space'=64,'chan'=8] {'chan'}, dimensions={0} | all-to-all | bytes 1585152 | tf_op jit(solution)/shard_map/all_to_all | solution.py:98
  102.0 0.5 reshape.251
  103.0 0.4 copy.430
  103.4 0.3 copy.445
  103.8 0.4 copy.485
  104.2 0.2 fusion.4
  105.0 1.0 pad_maximum_fusion.1
  106.0 7.1 %all-to-all-start.3 = ((bf16[64,38,128]{2,1,0:T(8,128)(2,1)}), bf16[64,38,128]{2,1,0:T(8,128)(2,1)S(1)}, u32[]{:S(2)}, u32[]{:S(2)}) async-start(bf16[64,38,128]{2,1,0:T(8,128)(2,1)} %pad_maximum_fusion.1), calls=%async_computation.3 | async-start | bytes 1310720 | tf_op jit(solution)/shard_map/all_to_all | solution.py:98
  113.1 0.6 copy.492
  113.7 19.4 %all-to-all-done.3 = bf16[64,38,128]{2,1,0:T(8,128)(2,1)S(1)} async-done(((bf16[64,38,128]{2,1,0:T(8,128)(2,1)}), bf16[64,38,128]{2,1,0:T(8,128)(2,1)S(1)}, u32[]{:S(2)}, u32[]{:S(2)}) %all-to-all-start.3) | async-done | bytes 622624 | tf_op jit(solution)/shard_map/all_to_all | solution.py:98
  133.2 0.7 broadcast_in_dim.53
  133.9 6.3 %all-to-all-start.4 = ((f32[64,3,128]{2,1,0:T(4,128)}), f32[64,3,128]{2,1,0:T(4,128)S(1)}, u32[]{:S(2)}, u32[]{:S(2)}) async-start(f32[64,3,128]{2,1,0:T(4,128)} %broadcast_in_dim.53), calls=%async_computation.4 | async-start | bytes 262144 | tf_op jit(solution)/shard_map/all_to_all | solution.py:98
  140.2 0.4 reshape_reshape_reshape_reshape.7
  140.6 0.6 gather_fusion.1
  141.5 0.3 copy.433
  141.8 0.3 copy.434
  142.1 0.5 fusion.6
  142.6 0.3 copy.435
  142.9 0.9 reshape.218
  143.8 6.7 %all-to-all-done.4 = f32[64,3,128]{2,1,0:T(4,128)S(1)} async-done(((f32[64,3,128]{2,1,0:T(4,128)}), f32[64,3,128]{2,1,0:T(4,128)S(1)}, u32[]{:S(2)}, u32[]{:S(2)}) %all-to-all-start.4) | async-done | bytes 98336 | tf_op jit(solution)/shard_map/all_to_all | solution.py:98
  150.6 0.6 slice.255
  151.4 0.6 slice_bitcast_fusion.2
  (110 shorter events, 4.4 us)
Async XLA Ops:
  0.6 14.9 %copy-start = (bf16[2,16,1024]{2,1,0:T(8,128)(2,1)S(1)}, bf16[2,16,1024]{2,1,0:T(8,128)(2,1)}, u32[]{:S(2)}) copy-start(bf16[2,16,1024]{2,1,0:T(8,128)(2,1)} %param.11) | copy-start | bytes 196612
  1.9 13.2 %copy-start.5 = (s32[2,4]{1,0:T(2,128)S(1)}, s32[2,4]{1,0:T(2,128)}, u32[]{:S(2)}) copy-start(s32[2,4]{1,0:T(2,128)} %param.12) | copy-start | bytes 100
  1.9 13.2 %copy-start.2 = (bf16[16,4,128]{2,1,0:T(4,128)(2,1)S(1)}, bf16[16,4,128]{2,1,0:T(4,128)(2,1)}, u32[]{:S(2)}) copy-start(bf16[16,4,128]{2,1,0:T(4,128)(2,1)} %param.10) | copy-start | bytes 49156
  1.9 13.2 %copy-start.1 = (bf16[16,9,64]{2,0,1:T(8,128)(2,1)S(1)}, bf16[16,9,64]{2,0,1:T(8,128)(2,1)}, u32[]{:S(2)}) copy-start(bf16[16,9,64]{2,0,1:T(8,128)(2,1)} %param.9) | copy-start | bytes 55300
  2.4 13.1 %copy-start.6 = (s32[2,4]{1,0:T(2,128)S(1)}, s32[2,4]{1,0:T(2,128)}, u32[]{:S(2)}) copy-start(s32[2,4]{1,0:T(2,128)} %param.13) | copy-start | bytes 100
  3.4 28.9 %all-to-all-start = ((bf16[64,32,128]{2,1,0:T(8,128)(2,1)}), bf16[64,32,128]{2,1,0:T(8,128)(2,1)S(1)}, u32[]{:S(2)}, u32[]{:S(2)}) async-start(bf16[64,32,128]{2,1,0:T(8,128)(2,1)} %broadcast_in_dim.51), calls=%async_computation | async-start | bytes 1048576 | tf_op jit(solution)/shard_map/all_to_all | solution.py:98
  66.2 1.3 copy-start.4
  67.5 0.7 copy-start.3
  70.8 0.7 copy-start.7
  106.0 27.2 %all-to-all-start.3 = ((bf16[64,38,128]{2,1,0:T(8,128)(2,1)}), bf16[64,38,128]{2,1,0:T(8,128)(2,1)S(1)}, u32[]{:S(2)}, u32[]{:S(2)}) async-start(bf16[64,38,128]{2,1,0:T(8,128)(2,1)} %pad_maximum_fusion.1), calls=%async_computation.3 | async-start | bytes 1310720 | tf_op jit(solution)/shard_map/all_to_all | solution.py:98
  133.9 16.6 %all-to-all-start.4 = ((f32[64,3,128]{2,1,0:T(4,128)}), f32[64,3,128]{2,1,0:T(4,128)S(1)}, u32[]{:S(2)}, u32[]{:S(2)}) async-start(f32[64,3,128]{2,1,0:T(4,128)} %broadcast_in_dim.53), calls=%async_computation.4 | async-start | bytes 262144 | tf_op jit(solution)/shard_map/all_to_all | solution.py:98

commit v11 on v10

--- a/solution.py
+++ b/solution.py
@@ -169,11 +169,9 @@
         dimension_numbers=swapped, preferred_element_type=F32,
     )
     down_part = down_part.transpose(1, 2, 3, 0).reshape(out_channels, down_cols)
-    w_up = jnp.flip(w_down, (2, 3)).transpose(1, 0, 2, 3)
-    grad_act = lax.conv_general_dilated(
-        grad_band, w_up, (1, 1), ((1, 1), (1, 1)), lhs_dilation=(2, 2),
-        dimension_numbers=plain, preferred_element_type=F32,
-    )
+    taps = down_full.reshape(out_channels, 2, 2, out_channels)
+    grad_act = jnp.einsum("opqc,touv->tcupvq", taps, grad_band, preferred_element_type=F32)
+    grad_act = grad_act.reshape(tiles, out_channels, rows, S)
     grad_pre = (grad_act * silu_grad(pre_act)).astype(BF16)
     conv_part = lax.conv_general_dilated(
         block, grad_pre, (1, 1), "VALID", dimension_numbers=swapped, preferred_element_type=F32

time: 152 us -> 153 us (level)
  no operation moved by 1% of the time
where the time goes in v11:
time: 153 us; the launch traced here: 152 us
  blocking collectives  53.3 us (35%)
  waiting for transfers between devices  42.9 us (28%)
  starting transfers between devices  25 us (16%)
  local copies, waits for them, and re-layouts  20.1 us (13%)
  other arithmetic  4.81 us (3%)
  matrix products  4.55 us (3%)
  between operations  1.61 us (1%)
    all_to_all x2, blocking collectives, exchange(): got = lax.all_to_all(jnp.concatenate(flat, axis=1), axis, 0, 0, tiled=True)  53.3 us
    all_to_all x3, waiting for transfers between devices, exchange(): got = lax.all_to_all(jnp.concatenate(flat, axis=1), axis, 0, 0, tiled=True)  42.9 us
    all_to_all x3, starting transfers between devices, exchange(): got = lax.all_to_all(jnp.concatenate(flat, axis=1), axis, 0, 0, tiled=True)  25 us
  transfers between devices with their start and end apart: 3, of which 3 were waited for; matrix products, arithmetic and copies ran while one was open for 3% of the time, Pallas kernels for 0%

profile of v11, /device:TPU:1, one launch (start us, length us, event | category | flops | bytes accessed | tf_op | source)
XLA Modules:
  0.0 152.2 jit_solution(10734628716937363017)
XLA Ops:
  0.6 1.2 reshape.198
  1.9 0.5 slice_reduce_fusion.1
  2.5 0.9 broadcast_in_dim.51
  3.4 11.6 %all-to-all-start = ((bf16[64,32,128]{2,1,0:T(8,128)(2,1)}), bf16[64,32,128]{2,1,0:T(8,128)(2,1)S(1)}, u32[]{:S(2)}, u32[]{:S(2)}) async-start(bf16[64,32,128]{2,1,0:T(8,128)(2,1)} %broadcast_in_dim.51), calls=%async_computation | async-start | bytes 1048576 | tf_op jit(solution)/shard_map/all_to_all | solution.py:98
  15.6 16.7 %all-to-all-done = bf16[64,32,128]{2,1,0:T(8,128)(2,1)S(1)} async-done(((bf16[64,32,128]{2,1,0:T(8,128)(2,1)}), bf16[64,32,128]{2,1,0:T(8,128)(2,1)S(1)}, u32[]{:S(2)}, u32[]{:S(2)}) %all-to-all-start) | async-done | bytes 524320 | tf_op jit(solution)/shard_map/all_to_all | solution.py:98
  32.3 0.4 reshape_reshape_reshape_reshape.6
  32.7 0.6 gather_fusion
  33.6 0.2 copy.396
  33.8 0.2 copy.395
  34.1 0.8 fusion.32
  35.0 0.2 copy_bitcast_fusion.1
  35.1 0.4 reshape.203
  35.7 27.9 %all_to_all.25 = bf16[8,259,128]{2,1,0:T(8,128)(2,1)S(1)} all-to-all(bf16[8,259,128]{2,1,0:T(8,128)(2,1)S(1)} %pad_maximum_fusion.2), channel_id=1, replica_groups=mesh['space'=64,'chan'=8] {'chan'}, dimensions={0} | all-to-all | bytes 1060864 | tf_op jit(solution)/shard_map/all_to_all | solution.py:98
  63.8 0.3 reshape_reshape.23
  64.5 0.2 reshape.211
  64.7 0.2 copy.416
  64.9 0.6 reshape.206
  65.6 0.4 copy.423
  66.0 0.4 copy.457
  66.4 0.4 pad.50.clone
  66.8 0.5 fusion.15
  67.3 0.3 convolution_bitcast_fusion
  67.6 0.4 copy.420
  68.0 0.7 add_multiply_fusion
  68.7 0.2 copy.421
  69.1 1.7 %fusion.34 = f32[128,3,3,64]{3,0,2,1:T(8,128)S(1)} fusion(bf16[2,64,10,66]{1,0,3,2:T(2,128)(2,1)S(1)} %copy.423, bf16[2,128,8,64]{1,3,2,0:T(8,128)(2,1)S(1)} %fusion.14), kind=kOutput, calls=%fused_computation.73 | convolution fusion | flops 150994944 | bytes 726016 | tf_op jit(solution)/shard_map/transpose | solution.py:179
  70.8 0.2 reshape.213
  71.0 0.2 copy.458
  71.3 0.4 copy-done.6
  71.7 1.0 fusion
  72.7 0.1 copy.431
  72.9 0.2 reshape.243
  73.1 0.2 copy.432
  73.4 0.2 copy.433
  73.6 0.4 reshape.215
  74.1 0.2 broadcast_select_fusion
  74.7 0.3 convolution_convert_fusion
  75.0 0.2 copy.411
  75.2 0.2 reshape.209
  75.4 0.6 fusion.23
  76.1 0.2 copy.417
  76.3 0.2 reshape_reshape.27
  76.8 25.4 %all_to_all.26 = bf16[8,387,128]{2,1,0:T(8,128)(2,1)S(1)} all-to-all(bf16[8,387,128]{2,1,0:T(8,128)(2,1)S(1)} %pad_maximum_fusion), channel_id=1, replica_groups=mesh['space'=64,'chan'=8] {'chan'}, dimensions={0} | all-to-all | bytes 1585152 | tf_op jit(solution)/shard_map/all_to_all | solution.py:98
  102.2 0.5 reshape.248
  103.2 0.4 copy.439
  103.6 0.3 copy.460
  104.0 0.4 copy.509
  104.4 0.2 fusion.4
  105.2 1.0 pad_maximum_fusion.1
  106.2 7.1 %all-to-all-start.3 = ((bf16[64,38,128]{2,1,0:T(8,128)(2,1)}), bf16[64,38,128]{2,1,0:T(8,128)(2,1)S(1)}, u32[]{:S(2)}, u32[]{:S(2)}) async-start(bf16[64,38,128]{2,1,0:T(8,128)(2,1)} %pad_maximum_fusion.1), calls=%async_computation.3 | async-start | bytes 1310720 | tf_op jit(solution)/shard_map/all_to_all | solution.py:98
  113.3 0.6 copy.516
  113.9 19.4 %all-to-all-done.3 = bf16[64,38,128]{2,1,0:T(8,128)(2,1)S(1)} async-done(((bf16[64,38,128]{2,1,0:T(8,128)(2,1)}), bf16[64,38,128]{2,1,0:T(8,128)(2,1)S(1)}, u32[]{:S(2)}, u32[]{:S(2)}) %all-to-all-start.3) | async-done | bytes 622624 | tf_op jit(solution)/shard_map/all_to_all | solution.py:98
  133.5 0.7 broadcast_in_dim.53
  134.1 6.3 %all-to-all-start.4 = ((f32[64,3,128]{2,1,0:T(4,128)}), f32[64,3,128]{2,1,0:T(4,128)S(1)}, u32[]{:S(2)}, u32[]{:S(2)}) async-start(f32[64,3,128]{2,1,0:T(4,128)} %broadcast_in_dim.53), calls=%async_computation.4 | async-start | bytes 262144 | tf_op jit(solution)/shard_map/all_to_all | solution.py:98
  140.5 0.4 reshape_reshape_reshape_reshape.7
  140.9 0.6 gather_fusion.1
  141.7 0.3 copy.442
  142.0 0.3 copy.443
  142.3 0.5 fusion.6
  142.8 0.3 copy.444
  143.1 0.9 reshape.222
  144.0 6.7 %all-to-all-done.4 = f32[64,3,128]{2,1,0:T(4,128)S(1)} async-done(((f32[64,3,128]{2,1,0:T(4,128)}), f32[64,3,128]{2,1,0:T(4,128)S(1)}, u32[]{:S(2)}, u32[]{:S(2)}) %all-to-all-start.4) | async-done | bytes 98336 | tf_op jit(solution)/shard_map/all_to_all | solution.py:98
  150.8 0.6 slice.253
  151.6 0.6 slice_bitcast_fusion.2
  (108 shorter events, 4.5 us)
Async XLA Ops:
  0.6 14.9 %copy-start = (bf16[2,16,1024]{2,1,0:T(8,128)(2,1)S(1)}, bf16[2,16,1024]{2,1,0:T(8,128)(2,1)}, u32[]{:S(2)}) copy-start(bf16[2,16,1024]{2,1,0:T(8,128)(2,1)} %param.11) | copy-start | bytes 196612
  1.9 13.2 %copy-start.4 = (s32[2,4]{1,0:T(2,128)S(1)}, s32[2,4]{1,0:T(2,128)}, u32[]{:S(2)}) copy-start(s32[2,4]{1,0:T(2,128)} %param.12) | copy-start | bytes 100
  1.9 13.2 %copy-start.2 = (bf16[16,4,128]{2,1,0:T(4,128)(2,1)S(1)}, bf16[16,4,128]{2,1,0:T(4,128)(2,1)}, u32[]{:S(2)}) copy-start(bf16[16,4,128]{2,1,0:T(4,128)(2,1)} %param.10) | copy-start | bytes 49156
  1.9 13.2 %copy-start.1 = (bf16[16,9,64]{2,0,1:T(8,128)(2,1)S(1)}, bf16[16,9,64]{2,0,1:T(8,128)(2,1)}, u32[]{:S(2)}) copy-start(bf16[16,9,64]{2,0,1:T(8,128)(2,1)} %param.9) | copy-start | bytes 55300
  2.4 13.1 %copy-start.5 = (s32[2,4]{1,0:T(2,128)S(1)}, s32[2,4]{1,0:T(2,128)}, u32[]{:S(2)}) copy-start(s32[2,4]{1,0:T(2,128)} %param.13) | copy-start | bytes 100
  3.4 28.9 %all-to-all-start = ((bf16[64,32,128]{2,1,0:T(8,128)(2,1)}), bf16[64,32,128]{2,1,0:T(8,128)(2,1)S(1)}, u32[]{:S(2)}, u32[]{:S(2)}) async-start(bf16[64,32,128]{2,1,0:T(8,128)(2,1)} %broadcast_in_dim.51), calls=%async_computation | async-start | bytes 1048576 | tf_op jit(solution)/shard_map/all_to_all | solution.py:98
  67.3 0.7 copy-start.3
  71.0 0.7 copy-start.6
  106.2 27.2 %all-to-all-start.3 = ((bf16[64,38,128]{2,1,0:T(8,128)(2,1)}), bf16[64,38,128]{2,1,0:T(8,128)(2,1)S(1)}, u32[]{:S(2)}, u32[]{:S(2)}) async-start(bf16[64,38,128]{2,1,0:T(8,128)(2,1)} %pad_maximum_fusion.1), calls=%async_computation.3 | async-start | bytes 1310720 | tf_op jit(solution)/shard_map/all_to_all | solution.py:98
  134.1 16.6 %all-to-all-start.4 = ((f32[64,3,128]{2,1,0:T(4,128)}), f32[64,3,128]{2,1,0:T(4,128)S(1)}, u32[]{:S(2)}, u32[]{:S(2)}) async-start(f32[64,3,128]{2,1,0:T(4,128)} %broadcast_in_dim.53), calls=%async_computation.4 | async-start | bytes 262144 | tf_op jit(solution)/shard_map/all_to_all | solution.py:98

commit v12 on v10

--- a/solution.py
+++ b/solution.py
@@ -164,11 +164,9 @@
     pooled_rows = lax.conv_general_dilated(
         activated, w_down, (2, 2), "VALID", dimension_numbers=plain, preferred_element_type=F32
     ).astype(BF16)
-    down_part = lax.conv_general_dilated(
-        activated, grad_band, (1, 1), "VALID", rhs_dilation=(2, 2),
-        dimension_numbers=swapped, preferred_element_type=F32,
-    )
-    down_part = down_part.transpose(1, 2, 3, 0).reshape(out_channels, down_cols)
+    quads = activated.reshape(tiles, out_channels, rows // 2, 2, half, 2)
+    down_part = jnp.einsum("touv,tcupvq->opqc", grad_band, quads, preferred_element_type=F32)
+    down_part = down_part.reshape(out_channels, down_cols)
     w_up = jnp.flip(w_down, (2, 3)).transpose(1, 0, 2, 3)
     grad_act = lax.conv_general_dilated(
         grad_band, w_up, (1, 1), ((1, 1), (1, 1)), lhs_dilation=(2, 2),

time: 152 us -> 152 us (level)
  no operation moved by 1% of the time
where the time goes in v12:
time: 152 us
  blocking collectives  53.3 us (35%)
  waiting for transfers between devices  42.9 us (28%)
  starting transfers between devices  25 us (16%)
  local copies, waits for them, and re-layouts  19.9 us (13%)
  other arithmetic  4.7 us (3%)
  matrix products  4.34 us (3%)
  between operations  1.61 us (1%)
    all_to_all x2, blocking collectives, exchange(): got = lax.all_to_all(jnp.concatenate(flat, axis=1), axis, 0, 0, tiled=True)  53.3 us
    all_to_all x3, waiting for transfers between devices, exchange(): got = lax.all_to_all(jnp.concatenate(flat, axis=1), axis, 0, 0, tiled=True)  42.9 us
    all_to_all x3, starting transfers between devices, exchange(): got = lax.all_to_all(jnp.concatenate(flat, axis=1), axis, 0, 0, tiled=True)  25 us
  transfers between devices with their start and end apart: 3, of which 3 were waited for; matrix products, arithmetic and copies ran while one was open for 3% of the time, Pallas kernels for 0%

profile of v12, /device:TPU:1, one launch (start us, length us, event | category | flops | bytes accessed | tf_op | source)
XLA Modules:
  0.0 151.7 jit_solution(15126792380480533435)
XLA Ops:
  0.6 1.2 reshape.198
  1.9 0.5 slice_reduce_fusion.1
  2.5 0.9 broadcast_in_dim.51
  3.4 11.6 %all-to-all-start = ((bf16[64,32,128]{2,1,0:T(8,128)(2,1)}), bf16[64,32,128]{2,1,0:T(8,128)(2,1)S(1)}, u32[]{:S(2)}, u32[]{:S(2)}) async-start(bf16[64,32,128]{2,1,0:T(8,128)(2,1)} %broadcast_in_dim.51), calls=%async_computation | async-start | bytes 1048576 | tf_op jit(solution)/shard_map/all_to_all | solution.py:98
  15.6 16.7 %all-to-all-done = bf16[64,32,128]{2,1,0:T(8,128)(2,1)S(1)} async-done(((bf16[64,32,128]{2,1,0:T(8,128)(2,1)}), bf16[64,32,128]{2,1,0:T(8,128)(2,1)S(1)}, u32[]{:S(2)}, u32[]{:S(2)}) %all-to-all-start) | async-done | bytes 524320 | tf_op jit(solution)/shard_map/all_to_all | solution.py:98
  32.3 0.4 reshape_reshape_reshape_reshape.6
  32.7 0.6 gather_fusion
  33.6 0.2 copy.395
  33.8 0.2 copy.394
  34.1 0.8 fusion.32
  34.9 0.2 copy_bitcast_fusion.1
  35.1 0.4 reshape.203
  35.7 27.9 %all_to_all.25 = bf16[8,259,128]{2,1,0:T(8,128)(2,1)S(1)} all-to-all(bf16[8,259,128]{2,1,0:T(8,128)(2,1)S(1)} %pad_maximum_fusion.2), channel_id=1, replica_groups=mesh['space'=64,'chan'=8] {'chan'}, dimensions={0} | all-to-all | bytes 1060864 | tf_op jit(solution)/shard_map/all_to_all | solution.py:98
  63.8 0.3 reshape_reshape.22
  64.5 0.2 reshape.212
  64.7 0.1 copy.457
  64.9 0.6 reshape.206
  65.6 0.4 copy.422
  66.0 0.4 copy.456
  66.4 0.4 pad.50.clone
  66.8 0.5 fusion.14
  67.3 0.3 convolution_select_fusion.1
  67.6 0.4 copy.420
  68.0 0.7 add_multiply_fusion
  68.7 0.2 copy.421
  69.0 1.6 %fusion.35 = f32[128,3,3,64]{3,0,2,1:T(8,128)S(1)} fusion(bf16[2,64,10,66]{1,0,3,2:T(2,128)(2,1)S(1)} %copy.422, bf16[8,2,64,128]{3,0,2,1:T(8,128)(2,1)S(1)} %fusion.7), kind=kOutput, calls=%fused_computation.74 | convolution fusion | flops 150994944 | bytes 726016 | tf_op jit(solution)/shard_map/transpose | solution.py:179
  70.7 0.2 reshape.213
  71.0 0.4 copy-done.7
  71.3 1.0 fusion
  72.4 0.1 copy.430
  72.5 0.2 reshape.250
  72.8 0.2 copy.431
  73.0 0.2 copy.432
  73.3 0.4 reshape.215
  73.8 0.2 broadcast_select_fusion
  74.3 0.2 convolution_convert_fusion
  74.6 0.2 copy.410
  74.8 0.2 reshape.209
  75.1 0.5 convolution_bitcast_fusion
  75.6 0.2 copy.417
  75.8 0.2 reshape_reshape.26
  76.1 0.1 reduce-precision_convert_fusion
  76.3 25.4 %all_to_all.26 = bf16[8,387,128]{2,1,0:T(8,128)(2,1)S(1)} all-to-all(bf16[8,387,128]{2,1,0:T(8,128)(2,1)S(1)} %pad_maximum_fusion), channel_id=1, replica_groups=mesh['space'=64,'chan'=8] {'chan'}, dimensions={0} | all-to-all | bytes 1585152 | tf_op jit(solution)/shard_map/all_to_all | solution.py:98
  101.8 0.5 reshape.255
  102.7 0.4 copy.438
  103.1 0.3 copy.459
  103.6 0.4 copy.501
  103.9 0.2 fusion.4
  104.7 1.0 pad_maximum_fusion.1
  105.7 7.1 %all-to-all-start.3 = ((bf16[64,38,128]{2,1,0:T(8,128)(2,1)}), bf16[64,38,128]{2,1,0:T(8,128)(2,1)S(1)}, u32[]{:S(2)}, u32[]{:S(2)}) async-start(bf16[64,38,128]{2,1,0:T(8,128)(2,1)} %pad_maximum_fusion.1), calls=%async_computation.3 | async-start | bytes 1310720 | tf_op jit(solution)/shard_map/all_to_all | solution.py:98
  112.8 0.6 copy.508
  113.4 19.4 %all-to-all-done.3 = bf16[64,38,128]{2,1,0:T(8,128)(2,1)S(1)} async-done(((bf16[64,38,128]{2,1,0:T(8,128)(2,1)}), bf16[64,38,128]{2,1,0:T(8,128)(2,1)S(1)}, u32[]{:S(2)}, u32[]{:S(2)}) %all-to-all-start.3) | async-done | bytes 622624 | tf_op jit(solution)/shard_map/all_to_all | solution.py:98
  133.0 0.7 broadcast_in_dim.53
  133.7 6.3 %all-to-all-start.4 = ((f32[64,3,128]{2,1,0:T(4,128)}), f32[64,3,128]{2,1,0:T(4,128)S(1)}, u32[]{:S(2)}, u32[]{:S(2)}) async-start(f32[64,3,128]{2,1,0:T(4,128)} %broadcast_in_dim.53), calls=%async_computation.4 | async-start | bytes 262144 | tf_op jit(solution)/shard_map/all_to_all | solution.py:98
  140.0 0.4 reshape_reshape_reshape_reshape.7
  140.4 0.6 gather_fusion.1
  141.2 0.3 copy.441
  141.5 0.3 copy.442
  141.9 0.5 fusion.6
  142.3 0.3 copy.443
  142.6 0.9 reshape.222
  143.6 6.7 %all-to-all-done.4 = f32[64,3,128]{2,1,0:T(4,128)S(1)} async-done(((f32[64,3,128]{2,1,0:T(4,128)}), f32[64,3,128]{2,1,0:T(4,128)S(1)}, u32[]{:S(2)}, u32[]{:S(2)}) %all-to-all-start.4) | async-done | bytes 98336 | tf_op jit(solution)/shard_map/all_to_all | solution.py:98
  150.3 0.6 slice.256
  151.1 0.6 slice_bitcast_fusion.2
  (110 shorter events, 4.3 us)
Async XLA Ops:
  0.6 14.9 %copy-start = (bf16[2,16,1024]{2,1,0:T(8,128)(2,1)S(1)}, bf16[2,16,1024]{2,1,0:T(8,128)(2,1)}, u32[]{:S(2)}) copy-start(bf16[2,16,1024]{2,1,0:T(8,128)(2,1)} %param.11) | copy-start | bytes 196612
  1.9 13.2 %copy-start.5 = (s32[2,4]{1,0:T(2,128)S(1)}, s32[2,4]{1,0:T(2,128)}, u32[]{:S(2)}) copy-start(s32[2,4]{1,0:T(2,128)} %param.12) | copy-start | bytes 100
  1.9 13.2 %copy-start.2 = (bf16[16,4,128]{2,1,0:T(4,128)(2,1)S(1)}, bf16[16,4,128]{2,1,0:T(4,128)(2,1)}, u32[]{:S(2)}) copy-start(bf16[16,4,128]{2,1,0:T(4,128)(2,1)} %param.10) | copy-start | bytes 49156
  1.9 13.2 %copy-start.1 = (bf16[16,9,64]{2,0,1:T(8,128)(2,1)S(1)}, bf16[16,9,64]{2,0,1:T(8,128)(2,1)}, u32[]{:S(2)}) copy-start(bf16[16,9,64]{2,0,1:T(8,128)(2,1)} %param.9) | copy-start | bytes 55300
  2.4 13.1 %copy-start.6 = (s32[2,4]{1,0:T(2,128)S(1)}, s32[2,4]{1,0:T(2,128)}, u32[]{:S(2)}) copy-start(s32[2,4]{1,0:T(2,128)} %param.13) | copy-start | bytes 100
  3.4 28.9 %all-to-all-start = ((bf16[64,32,128]{2,1,0:T(8,128)(2,1)}), bf16[64,32,128]{2,1,0:T(8,128)(2,1)S(1)}, u32[]{:S(2)}, u32[]{:S(2)}) async-start(bf16[64,32,128]{2,1,0:T(8,128)(2,1)} %broadcast_in_dim.51), calls=%async_computation | async-start | bytes 1048576 | tf_op jit(solution)/shard_map/all_to_all | solution.py:98
  66.0 1.3 copy-start.4
  67.3 0.7 copy-start.3
  70.7 0.7 copy-start.7
  105.7 27.2 %all-to-all-start.3 = ((bf16[64,38,128]{2,1,0:T(8,128)(2,1)}), bf16[64,38,128]{2,1,0:T(8,128)(2,1)S(1)}, u32[]{:S(2)}, u32[]{:S(2)}) async-start(bf16[64,38,128]{2,1,0:T(8,128)(2,1)} %pad_maximum_fusion.1), calls=%async_computation.3 | async-start | bytes 1310720 | tf_op jit(solution)/shard_map/all_to_all | solution.py:98
  133.7 16.6 %all-to-all-start.4 = ((f32[64,3,128]{2,1,0:T(4,128)}), f32[64,3,128]{2,1,0:T(4,128)S(1)}, u32[]{:S(2)}, u32[]{:S(2)}) async-start(f32[64,3,128]{2,1,0:T(4,128)} %broadcast_in_dim.53), calls=%async_computation.4 | async-start | bytes 262144 | tf_op jit(solution)/shard_map/all_to_all | solution.py:98
